TPU v7x, 768 devices: a whole 4x8x12 slice. The times are simulated.
768 devices in a mesh: fsdp: 12 (over z), tensor: 64 (over y, x, core).
Axes of the slice: x: 4, y: 8, z: 12, core: 2. Of those that a mesh axis runs over, the one named last changes fastest.
Arguments:
- momentum: float32 [1536, 24576], P('fsdp', 'tensor'), may hold values from -6 to 6
- gradient: bfloat16 [1536, 24576], P('fsdp', 'tensor'), may hold values from -6 to 6
- weight: bfloat16 [1536, 24576], P('fsdp', 'tensor'), may hold values from -6 to 6
- basis: float32 [24576, 512], P('tensor'), may hold values from -0.0390625 to 0.0390625
Outputs:
- new_momentum: float32 [1536, 24576], P('fsdp', 'tensor')
- new_basis: float32 [24576, 512], P('tensor')
- new_weight: bfloat16 [1536, 24576], P('fsdp', 'tensor')
All inputs are finite; a program needn't handle non-finite values.
Results may differ from a plain program's by a relative error of at most 0.001.
Values sent between devices are 32-bit elements; how exact they have to be, the bound alone decides.
No kernel may reach another device: no remote copies, remote signals or barrier semaphores. Data moves between devices by JAX's collectives and lax.ppermute only.
A program may use at most 32 MiB of HBM per device.

v0:
```python
import jax
import jax.numpy as jnp
from jax import lax
from jax.sharding import PartitionSpec as P


def local(momentum, gradient, weight, basis):
    highest = lax.Precision.HIGHEST
    buffer = momentum + gradient.astype(jnp.float32)
    panel_part = jnp.dot(buffer, basis, precision=highest)
    panel_full = lax.psum(panel_part, "tensor")
    gram_matrix = lax.psum(jnp.dot(panel_full.T, panel_full, precision=highest), "fsdp")
    factor = jnp.linalg.cholesky(gram_matrix)
    orthonormal = lax.linalg.triangular_solve(
        factor, panel_full, left_side=False, lower=True, transpose_a=True
    )
    right_part = jnp.dot(buffer.T, orthonormal, precision=highest)
    right_factor = lax.psum(right_part, "fsdp")
    col_sumsq = lax.psum(jnp.sum(right_factor * right_factor, axis=0), "tensor")
    new_basis = right_factor / jnp.sqrt(col_sumsq + 1e-06)
    new_momentum = buffer - 0.1 * jnp.dot(orthonormal, right_factor.T, precision=highest)
    total_rows = buffer.shape[0] * lax.axis_size("fsdp")
    total_cols = buffer.shape[1] * lax.axis_size("tensor")
    step_scale = 0.2 * jnp.sqrt(jnp.float32(total_rows * total_cols / basis.shape[1]))
    update = jnp.dot(orthonormal, new_basis.T, precision=highest)
    new_weight = (weight.astype(jnp.float32) - step_scale * update).astype(jnp.bfloat16)
    return (new_momentum, new_basis, new_weight)


def solution(mesh):
    placed = (P("fsdp", "tensor"), P("fsdp", "tensor"), P("fsdp", "tensor"), P("tensor", None))
    return jax.shard_map(
        local,
        mesh=mesh,
        in_specs=placed,
        out_specs=(P("fsdp", "tensor"), P("tensor", None), P("fsdp", "tensor")),
        check_vma=False,
    )
```

profile of v0, /device:TPU:1, one launch (start us, length us, event | category | flops | bytes accessed | tf_op | source)
XLA Modules:
  0.0 719.7 jit_solution(1545123352573721542)
XLA Ops:
  7.2 1.1 copy-done
  8.3 2.3 fusion.21
  10.7 206.5 %all-reduce.5.cloned.1.call-done = f32[128,512]{1,0:T(8,128)} async-done(((f32[128,512]{1,0:T(8,128)}), f32[128,512]{1,0:T(8,128)}) %all-reduce.5.cloned.1.call-update) | async-done | bytes 262160 | tf_op jit(solution)/shard_map/psum | solution.py:11
  217.2 3.1 fusion.39
  220.4 106.2 %all-reduce.7.cloned.1.call-done = f32[512,512]{0,1:T(8,128)} async-done(((f32[512,512]{0,1:T(8,128)}), f32[512,512]{0,1:T(8,128)}) %all-reduce.7.cloned.1.call-update) | async-done | bytes 1048592 | tf_op jit(solution)/shard_map/psum | solution.py:12
  326.5 1.6 copy.8
  328.4 1.0 copy-done.4
  329.4 11.7 %cholesky.104 = f32[128,128]{1,0:T(8,128)S(1)} custom-call(f32[128,128]{1,0:T(8,128)S(1)} %cholesky.266), custom_call_target="Cholesky" | custom-call | tf_op jit(solution)/shard_map/jit(cholesky)/cholesky | solution.py:13
  341.2 9.8 %custom-call.30 = f32[1,128,128]{1,2,0:T(8,128)S(1)} custom-call(f32[1,128,128]{2,1,0:T(8,128)S(1)} %get-tuple-element.30), custom_call_target="InvertDiagBlocksLowerTriangular" | custom-call | tf_op jit(solution)/shard_map/jit(cholesky)/cholesky | solution.py:13
  351.8 11.7 %cholesky.217 = f32[128,128]{1,0:T(8,128)S(1)} custom-call(f32[128,128]{1,0:T(8,128)S(1)} %cholesky.270), custom_call_target="Cholesky" | custom-call | tf_op jit(solution)/shard_map/jit(cholesky)/cholesky | solution.py:13
  363.5 9.9 %custom-call.31 = f32[1,128,128]{1,2,0:T(8,128)S(1)} custom-call(f32[1,128,128]{2,1,0:T(8,128)S(1)} %get-tuple-element.27), custom_call_target="InvertDiagBlocksLowerTriangular" | custom-call | tf_op jit(solution)/shard_map/jit(cholesky)/cholesky | solution.py:13
  374.2 11.7 %cholesky.238 = f32[128,128]{1,0:T(8,128)S(1)} custom-call(f32[128,128]{1,0:T(8,128)S(1)} %cholesky.275), custom_call_target="Cholesky" | custom-call | tf_op jit(solution)/shard_map/jit(cholesky)/cholesky | solution.py:13
  385.9 0.7 compare_reduce_fusion.1
  386.6 9.8 %custom-call.32 = f32[1,128,128]{1,2,0:T(8,128)S(1)} custom-call(f32[1,128,128]{2,1,0:T(8,128)S(1)} %get-tuple-element.24), custom_call_target="InvertDiagBlocksLowerTriangular" | custom-call | tf_op jit(solution)/shard_map/jit(cholesky)/cholesky | solution.py:13
  397.1 11.7 %cholesky.255 = f32[128,128]{1,0:T(8,128)S(1)} custom-call(f32[128,128]{1,0:T(8,128)S(1)} %convolution_subtract_fusion.5), custom_call_target="Cholesky" | custom-call | tf_op jit(solution)/shard_map/jit(cholesky)/cholesky | solution.py:13
  408.8 0.6 compare_reduce_fusion
  409.4 0.6 compare_reduce_fusion.2
  413.0 8.0 %while.1 = (s32[]{:T(128)}, f32[512,512]{1,0:T(8,128)S(1)}, s32[4,2]{0,1:T(2,128)S(1)}, f32[4,128,128]{2,1,0:T(8,128)S(1)}, s32[]{:T(128)}) while((s32[]{:T(128)}, f32[512,512]{1,0:T(8,128)S(1)}, s32[4,2]{0,1:T(2,128)S(1)}, f32[4,128,128]{2,1,0:T(8,128)S(1)}, s32[]{:T(128)}) %tuple.31), condition=%wide.while_cond, body=%wide.while_body.sunk | while | flops 2 | bytes 131181 | solution.py:14
  413.6 1.4 bitcast_dynamic-update-slice_fusion.2
  415.1 0.5 fusion.51
  415.6 1.4 bitcast_dynamic-update-slice_fusion.2
  417.6 1.4 bitcast_dynamic-update-slice_fusion.2
  419.6 1.4 bitcast_dynamic-update-slice_fusion.2
  421.0 39.3 %custom-call.33 = f32[4,128,128]{1,2,0:T(8,128)S(1)} custom-call(f32[4,128,128]{2,1,0:T(8,128)S(1)} %get-tuple-element.10), custom_call_target="InvertDiagBlocksLowerTriangular" | custom-call | tf_op jit(solution)/shard_map/triangular_solve | solution.py:14
  462.8 0.6 copy-done.7
  463.4 1.7 fusion.20
  465.1 110.9 %all-reduce.9.cloned.1.call-done = f32[384,512]{1,0:T(8,128)} async-done(((f32[384,512]{1,0:T(8,128)}), f32[384,512]{1,0:T(8,128)}) %all-reduce.9.cloned.1.call-update) | async-done | bytes 786448 | tf_op jit(solution)/shard_map/psum | solution.py:18
  576.0 1.3 multiply_reduce_fusion
  577.3 131.5 %psum.31 = f32[512]{0:T(512)S(1)} all-reduce(f32[512]{0:T(512)S(1)} %multiply_reduce_fusion), channel_id=1, replica_groups=mesh['fsdp'=12,'tensor'=64] {'tensor'}, use_global_device_ids=true, to_apply=%region_12.13 | all-reduce | flops 512 | bytes 4096 | tf_op jit(solution)/shard_map/psum | solution.py:19
  709.0 0.8 copy-done.9
  709.8 1.7 fusion.2
  711.4 1.7 fusion
  (57 shorter events, 7.3 us)
Async XLA Ops:
  7.2 1.1 copy-start
  7.2 210.0 %all-reduce.5.cloned.1.call-start = ((), (), s32[]{:S(2)}) async-start(), calls=%async_computation | async-start | bytes 524288 | tf_op jit(solution)/shard_map/psum | solution.py:11
  10.7 315.9 %all-reduce.7.cloned.1.call-start = ((), (), s32[]{:S(2)}) async-start(), calls=%async_computation.1 | async-start | bytes 2097152 | tf_op jit(solution)/shard_map/psum | solution.py:12
  220.3 355.7 %all-reduce.9.cloned.1.call-start = ((), (), s32[]{:S(2)}) async-start(), calls=%async_computation.2 | async-start | bytes 1572864 | tf_op jit(solution)/shard_map/psum | solution.py:18
  326.5 1.7 copy-start.2
  328.4 1.0 copy-start.4
  329.4 21.7 %copy-start.5 = (f32[512,512]{1,0:T(8,128)S(1)}, f32[512,512]{1,0:T(8,128)}, u32[]{:S(2)}) copy-start(f32[512,512]{1,0:T(8,128)} %copy-done.4) | copy-start | bytes 3145732
  412.6 47.7 %copy-start.6 = (f32[128,512]{1,0:T(8,128)S(1)}, f32[128,512]{1,0:T(8,128)}, u32[]{:S(2)}) copy-start(f32[128,512]{1,0:T(8,128)} %all-reduce.5.cloned.1.call-done) | copy-start | bytes 786436
  461.9 0.9 copy-start.8
  462.4 0.9 copy-start.7
  576.0 132.9 %copy-start.1 = (f32[384,512]{1,0:T(8,128)S(1)}, f32[384,512]{1,0:T(8,128)}, u32[]{:S(2)}) copy-start(f32[384,512]{1,0:T(8,128)} %all-reduce.9.cloned.1.call-done) | copy-start | bytes 2359300
  708.8 0.9 copy-start.9
  709.7 3.4 copy-start.3
Sparse Core Ops, SparseCore 0:
  12.1 205.0 all-reduce.4
  220.4 106.0 all-reduce.6
  465.2 110.7 all-reduce.8
where the time goes:
time: 720 us
  waiting for transfers between devices  424 us (59%)
  blocking collectives  132 us (18%)
  other arithmetic  120 us (17%)
  between operations  16.6 us (2%)
  matrix products  14.7 us (2%)
  local copies, waits for them, and re-layouts  13.2 us (2%)
    psum x1, waiting for transfers between devices, local(): panel_full = lax.psum(panel_part, 'tensor')  206 us
    psum x1, blocking collectives, local(): col_sumsq = lax.psum(jnp.sum(right_factor * right_factor, axis=0), 'tensor')  132 us
    psum x1, waiting for transfers between devices, local(): right_factor = lax.psum(right_part, 'fsdp')  111 us
    psum x1, waiting for transfers between devices, local(): lax.psum(jnp.dot(panel_full.T, panel_full, precision=highest), 'fsdp')  106 us
    another operation x14, other arithmetic, local(): factor = jnp.linalg.cholesky(gram_matrix)  78.5 us
    another operation x3, other arithmetic, local(): lax.linalg.triangular_solve(factor, panel_full, left_side=False, lower=Tr...  39.7 us
  transfers between devices with their start and end apart: 3, of which 3 were waited for; matrix products, arithmetic and copies ran while one was open for 0% of the time, Pallas kernels for 0%

commit v1 on v0

--- a/solution.py
+++ b/solution.py
@@ -4,19 +4,34 @@
 from jax.sharding import PartitionSpec as P
 
 
+def xor_psum(x, axis, size):
+    step = 1
+    while step < size:
+        x = x + lax.ppermute(x, axis, [(i, i ^ step) for i in range(size)])
+        step *= 2
+    return x
+
+
 def local(momentum, gradient, weight, basis):
     highest = lax.Precision.HIGHEST
+    rank = basis.shape[1]
     buffer = momentum + gradient.astype(jnp.float32)
     panel_part = jnp.dot(buffer, basis, precision=highest)
-    panel_full = lax.psum(panel_part, "tensor")
-    gram_matrix = lax.psum(jnp.dot(panel_full.T, panel_full, precision=highest), "fsdp")
+    tensor_size = lax.axis_size("tensor")
+    panel_full = xor_psum(panel_part, "tensor", tensor_size)
+    gram_part = jnp.dot(panel_full.T, panel_full, precision=highest)
+    cross_part = jnp.dot(buffer.T, panel_full, precision=highest)
+    merged = lax.psum(jnp.concatenate([gram_part, cross_part], axis=0), "fsdp")
+    gram_matrix = merged[:rank]
+    cross = merged[rank:]
     factor = jnp.linalg.cholesky(gram_matrix)
-    orthonormal = lax.linalg.triangular_solve(
-        factor, panel_full, left_side=False, lower=True, transpose_a=True
+    rows = panel_full.shape[0]
+    solved = lax.linalg.triangular_solve(
+        factor, jnp.concatenate([panel_full, cross], axis=0), left_side=False, lower=True, transpose_a=True
     )
-    right_part = jnp.dot(buffer.T, orthonormal, precision=highest)
-    right_factor = lax.psum(right_part, "fsdp")
-    col_sumsq = lax.psum(jnp.sum(right_factor * right_factor, axis=0), "tensor")
+    orthonormal = solved[:rows]
+    right_factor = solved[rows:]
+    col_sumsq = xor_psum(jnp.sum(right_factor * right_factor, axis=0), "tensor", tensor_size)
     new_basis = right_factor / jnp.sqrt(col_sumsq + 1e-06)
     new_momentum = buffer - 0.1 * jnp.dot(orthonormal, right_factor.T, precision=highest)
     total_rows = buffer.shape[0] * lax.axis_size("fsdp")

time: 720 us -> 405 us (0.56)
  waiting for transfers between devices: 424 us -> 167 us
  blocking collectives: 132 us -> 0 us
  starting transfers between devices: 0.12 us -> 53.8 us
  other arithmetic: 120 us -> 128 us
    psum x3 -> x1, waiting for transfers between devices: 424 us -> 111 us  [local(): merged = lax.psum(jnp.concatenate([gram_part, cross_part], axis=0), 'fsdp')]
    psum x1 -> x0, blocking collectives: 132 us -> none  [local(): col_sumsq = lax.psum(jnp.sum(right_factor * right_factor, axis=0), 'tensor')]
    ppermute x0 -> x12, waiting for transfers between devices: none -> 55.5 us  [xor_psum(): x = x + lax.ppermute(x, axis, [(i, i ^ step) for i in range(size)])]
    ppermute x0 -> x12, starting transfers between devices: none -> 53.8 us  [xor_psum(): x = x + lax.ppermute(x, axis, [(i, i ^ step) for i in range(size)])]
  transfers between devices with their start and end apart: 3 -> 13, of which waited for: 3 -> 12; matrix products, arithmetic and copies ran while one was open for 0% -> 0% of each run, Pallas kernels for 0% -> 0%
where the time goes in v1:
time: 405 us; the launch traced here: 400 us
  waiting for transfers between devices  167 us (41%)
  other arithmetic  128 us (32%)
  starting transfers between devices  53.8 us (13%)
  local copies, waits for them, and re-layouts  18.2 us (4%)
  between operations  17.1 us (4%)
  matrix products  15.4 us (4%)
    psum x1, waiting for transfers between devices, local(): merged = lax.psum(jnp.concatenate([gram_part, cross_part], axis=0), 'fsdp')  111 us
    another operation x14, other arithmetic, local(): factor = jnp.linalg.cholesky(gram_matrix)  84.9 us
    ppermute x12, waiting for transfers between devices, xor_psum(): x = x + lax.ppermute(x, axis, [(i, i ^ step) for i in range(size)])  55.5 us
    ppermute x12, starting transfers between devices, xor_psum(): x = x + lax.ppermute(x, axis, [(i, i ^ step) for i in range(size)])  53.8 us
    another operation x3, other arithmetic, local(): lax.linalg.triangular_solve(factor, jnp.concatenate([panel_full, cross],...  40.3 us
    another operation x12, local copies, waits for them, and re-layouts  10.4 us
  transfers between devices with their start and end apart: 13, of which 12 were waited for; matrix products, arithmetic and copies ran while one was open for 0% of the time, Pallas kernels for 0%

profile of v1, /device:TPU:1, one launch (start us, length us, event | category | flops | bytes accessed | tf_op | source)
XLA Modules:
  0.0 399.9 jit_solution(513313699502546455)
XLA Ops:
  8.3 2.5 fusion.38
  10.8 12.4 %collective-permute-start = (f32[128,512]{0,1:T(8,128)S(1)}, f32[128,512]{0,1:T(8,128)S(1)}, u32[]{:S(2)}, u32[]{:S(2)}) collective-permute-start(f32[128,512]{0,1:T(8,128)S(1)} %fusion.38), channel_id=1, source_target_pairs={{0,1},{1,0},{2,3},{3,2},{4,5},{5,4},{6,7},{7,6},{8,9},{9,8},{10,11... | collective-permute-start | bytes 786440 | tf_op jit(solution)/shard_map/ppermute | solution.py:10
  24.4 2.1 collective-permute-start.1
  26.5 7.5 %collective-permute-done.1 = f32[128,512]{0,1:T(8,128)S(1)} collective-permute-done((f32[128,512]{0,1:T(8,128)S(1)}, f32[128,512]{0,1:T(8,128)S(1)}, u32[]{:S(2)}, u32[]{:S(2)}) %collective-permute-start.1) | collective-permute-done | bytes 262176 | tf_op jit(solution)/shard_map/ppermute | solution.py:10
  34.0 1.9 collective-permute-start.2
  35.9 8.1 %collective-permute-done.2 = f32[128,512]{0,1:T(8,128)S(1)} collective-permute-done((f32[128,512]{0,1:T(8,128)S(1)}, f32[128,512]{0,1:T(8,128)S(1)}, u32[]{:S(2)}, u32[]{:S(2)}) %collective-permute-start.2) | collective-permute-done | bytes 262176 | tf_op jit(solution)/shard_map/ppermute | solution.py:10
  44.0 1.9 collective-permute-start.3
  45.9 5.6 %collective-permute-done.3 = f32[128,512]{0,1:T(8,128)S(1)} collective-permute-done((f32[128,512]{0,1:T(8,128)S(1)}, f32[128,512]{0,1:T(8,128)S(1)}, u32[]{:S(2)}, u32[]{:S(2)}) %collective-permute-start.3) | collective-permute-done | bytes 262176 | tf_op jit(solution)/shard_map/ppermute | solution.py:10
  51.6 1.9 collective-permute-start.4
  53.6 14.3 %collective-permute-done.4 = f32[128,512]{0,1:T(8,128)S(1)} collective-permute-done((f32[128,512]{0,1:T(8,128)S(1)}, f32[128,512]{0,1:T(8,128)S(1)}, u32[]{:S(2)}, u32[]{:S(2)}) %collective-permute-start.4) | collective-permute-done | bytes 262176 | tf_op jit(solution)/shard_map/ppermute | solution.py:10
  67.9 2.1 collective-permute-start.5
  70.0 13.2 %collective-permute-done.5 = f32[128,512]{0,1:T(8,128)S(1)} collective-permute-done((f32[128,512]{0,1:T(8,128)S(1)}, f32[128,512]{0,1:T(8,128)S(1)}, u32[]{:S(2)}, u32[]{:S(2)}) %collective-permute-start.5) | collective-permute-done | bytes 262176 | tf_op jit(solution)/shard_map/ppermute | solution.py:10
  86.5 111.4 %all-reduce.3.cloned.1.call-done = f32[896,512]{0,1:T(8,128)} async-done(((f32[896,512]{0,1:T(8,128)}), f32[896,512]{0,1:T(8,128)}) %all-reduce.3.cloned.1.call-update) | async-done | bytes 1835024 | tf_op jit(solution)/shard_map/psum | solution.py:24
  200.9 11.7 %cholesky.104 = f32[128,128]{1,0:T(8,128)S(1)} custom-call(f32[128,128]{1,0:T(8,128)S(1)} %cholesky.266), custom_call_target="Cholesky" | custom-call | tf_op jit(solution)/shard_map/jit(cholesky)/cholesky | solution.py:27
  213.4 10.6 %custom-call.30 = f32[1,128,128]{1,2,0:T(8,128)S(1)} custom-call(f32[1,128,128]{2,1,0:T(8,128)} %get-tuple-element.33), custom_call_target="InvertDiagBlocksLowerTriangular" | custom-call | tf_op jit(solution)/shard_map/jit(cholesky)/cholesky | solution.py:27
  226.0 12.7 %cholesky.217 = f32[128,128]{1,0:T(8,128)S(1)} custom-call(f32[128,128]{1,0:T(8,128)} %cholesky.270), custom_call_target="Cholesky" | custom-call | tf_op jit(solution)/shard_map/jit(cholesky)/cholesky | solution.py:27
  239.4 10.6 %custom-call.31 = f32[1,128,128]{1,2,0:T(8,128)S(1)} custom-call(f32[1,128,128]{2,1,0:T(8,128)} %get-tuple-element.30), custom_call_target="InvertDiagBlocksLowerTriangular" | custom-call | tf_op jit(solution)/shard_map/jit(cholesky)/cholesky | solution.py:27
  252.9 12.5 %cholesky.238 = f32[128,128]{1,0:T(8,128)S(1)} custom-call(f32[128,128]{1,0:T(8,128)} %cholesky.275), custom_call_target="Cholesky" | custom-call | tf_op jit(solution)/shard_map/jit(cholesky)/cholesky | solution.py:27
  266.1 10.6 %custom-call.32 = f32[1,128,128]{1,2,0:T(8,128)S(1)} custom-call(f32[1,128,128]{2,1,0:T(8,128)} %get-tuple-element.27), custom_call_target="InvertDiagBlocksLowerTriangular" | custom-call | tf_op jit(solution)/shard_map/jit(cholesky)/cholesky | solution.py:27
  278.2 12.0 %cholesky.255 = f32[128,128]{1,0:T(8,128)S(1)} custom-call(f32[128,128]{1,0:T(8,128)S(1)} %convolution_subtract_fusion.2), custom_call_target="Cholesky" | custom-call | tf_op jit(solution)/shard_map/jit(cholesky)/cholesky | solution.py:27
  294.9 10.5 %while.1 = (s32[]{:T(128)}, f32[512,512]{1,0:T(8,128)S(1)}, s32[4,2]{0,1:T(2,128)S(1)}, f32[4,128,128]{2,1,0:T(8,128)}, s32[]{:T(128)}) while((s32[]{:T(128)}, f32[512,512]{1,0:T(8,128)S(1)}, s32[4,2]{0,1:T(2,128)S(1)}, f32[4,128,128]{2,1,0:T(8,128)}, s32[]{:T(128)}) %tuple.32), condition=%wide.while_cond, body=%wide.while_body.sunk | while | flops 2 | bytes 132205 | solution.py:29
  295.5 2.0 bitcast_dynamic-update-slice_fusion.2
  298.1 2.0 bitcast_dynamic-update-slice_fusion.2
  300.8 2.0 bitcast_dynamic-update-slice_fusion.2
  303.4 2.0 bitcast_dynamic-update-slice_fusion.2
  305.4 40.1 %custom-call.33 = f32[4,128,128]{1,2,0:T(8,128)S(1)} custom-call(f32[4,128,128]{2,1,0:T(8,128)} %get-tuple-element.10), custom_call_target="InvertDiagBlocksLowerTriangular" | custom-call | tf_op jit(solution)/shard_map/triangular_solve | solution.py:29
  351.9 9.5 %collective-permute-start.6 = (f32[512]{0:T(512)S(1)}, f32[512]{0:T(512)S(1)}, u32[]{:S(2)}, u32[]{:S(2)}) collective-permute-start(f32[512]{0:T(512)S(1)} %multiply_reduce_fusion), channel_id=1, source_target_pairs={{0,1},{1,0},{2,3},{3,2},{4,5},{5,4},{6,7},{7,6},{8,9},{9,8},{10,11... | collective-permute-start | bytes 6152 | tf_op jit(solution)/shard_map/ppermute | solution.py:10
  362.2 3.1 collective-permute-start.7
  366.5 4.6 %collective-permute-start.8 = (f32[512]{0:T(512)S(1)}, f32[512]{0:T(512)S(1)}, u32[]{:S(2)}, u32[]{:S(2)}) collective-permute-start(f32[512]{0:T(512)S(1)} %add.96), channel_id=1, source_target_pairs={{0,4},{1,5},{2,6},{3,7},{4,0},{5,1},{6,2},{7,3},{8,12},{9,13},{10,... | collective-permute-start | bytes 6152 | tf_op jit(solution)/shard_map/ppermute | solution.py:10
  372.4 3.1 collective-permute-start.9
  376.7 4.0 %collective-permute-start.10 = (f32[512]{0:T(512)S(1)}, f32[512]{0:T(512)S(1)}, u32[]{:S(2)}, u32[]{:S(2)}) collective-permute-start(f32[512]{0:T(512)S(1)} %add.98), channel_id=1, source_target_pairs={{0,16},{1,17},{2,18},{3,19},{4,20},{5,21},{6,22},{7,23},{8,24},{9,... | collective-permute-start | bytes 6152 | tf_op jit(solution)/shard_map/ppermute | solution.py:10
  381.9 7.1 %collective-permute-start.11 = (f32[512]{0:T(512)S(1)}, f32[512]{0:T(512)S(1)}, u32[]{:S(2)}, u32[]{:S(2)}) collective-permute-start(f32[512]{0:T(512)S(1)} %add.99), channel_id=1, source_target_pairs={{0,32},{1,33},{2,34},{3,35},{4,36},{5,37},{6,38},{7,39},{8,40},{9,... | collective-permute-start | bytes 6152 | tf_op jit(solution)/shard_map/ppermute | solution.py:10
  (84 shorter events, 37.5 us)
Async XLA Ops:
  7.2 1.1 copy-start
  7.2 190.7 %all-reduce.3.cloned.1.call-start = ((), (), s32[]{:S(2)}) async-start(), calls=%async_computation | async-start | bytes 3670016 | tf_op jit(solution)/shard_map/psum | solution.py:24
  10.8 13.6 %collective-permute-start = (f32[128,512]{0,1:T(8,128)S(1)}, f32[128,512]{0,1:T(8,128)S(1)}, u32[]{:S(2)}, u32[]{:S(2)}) collective-permute-start(f32[128,512]{0,1:T(8,128)S(1)} %fusion.38), channel_id=1, source_target_pairs={{0,1},{1,0},{2,3},{3,2},{4,5},{5,4},{6,7},{7,6},{8,9},{9,8},{10,11... | collective-permute-start | bytes 786440 | tf_op jit(solution)/shard_map/ppermute | solution.py:10
  24.4 58.9 %copy-start.1 = (f32[128,384]{1,0:T(8,128)S(1)}, f32[128,384]{1,0:T(8,128)}, u32[]{:S(2)}) copy-start(f32[128,384]{1,0:T(8,128)} %param.4) | copy-start | bytes 589828
  24.4 58.9 %copy-start.2 = (bf16[128,384]{1,0:T(8,128)(2,1)S(1)}, bf16[128,384]{1,0:T(8,128)(2,1)}, u32[]{:S(2)}) copy-start(bf16[128,384]{1,0:T(8,128)(2,1)} %param.5) | copy-start | bytes 294916
  24.4 9.5 %collective-permute-start.1 = (f32[128,512]{0,1:T(8,128)S(1)}, f32[128,512]{0,1:T(8,128)S(1)}, u32[]{:S(2)}, u32[]{:S(2)}) collective-permute-start(f32[128,512]{0,1:T(8,128)S(1)} %add.88), channel_id=1, source_target_pairs={{0,2},{1,3},{2,0},{3,1},{4,6},{5,7},{6,4},{7,5},{8,10},{9,11},{10,... | collective-permute-start | bytes 786440 | tf_op jit(solution)/shard_map/ppermute | solution.py:10
  34.0 10.0 %collective-permute-start.2 = (f32[128,512]{0,1:T(8,128)S(1)}, f32[128,512]{0,1:T(8,128)S(1)}, u32[]{:S(2)}, u32[]{:S(2)}) collective-permute-start(f32[128,512]{0,1:T(8,128)S(1)} %add.89), channel_id=1, source_target_pairs={{0,4},{1,5},{2,6},{3,7},{4,0},{5,1},{6,2},{7,3},{8,12},{9,13},{10,... | collective-permute-start | bytes 786440 | tf_op jit(solution)/shard_map/ppermute | solution.py:10
  44.0 7.6 %collective-permute-start.3 = (f32[128,512]{0,1:T(8,128)S(1)}, f32[128,512]{0,1:T(8,128)S(1)}, u32[]{:S(2)}, u32[]{:S(2)}) collective-permute-start(f32[128,512]{0,1:T(8,128)S(1)} %add.90), channel_id=1, source_target_pairs={{0,8},{1,9},{2,10},{3,11},{4,12},{5,13},{6,14},{7,15},{8,0},{9,1},... | collective-permute-start | bytes 786440 | tf_op jit(solution)/shard_map/ppermute | solution.py:10
  51.6 16.2 %collective-permute-start.4 = (f32[128,512]{0,1:T(8,128)S(1)}, f32[128,512]{0,1:T(8,128)S(1)}, u32[]{:S(2)}, u32[]{:S(2)}) collective-permute-start(f32[128,512]{0,1:T(8,128)S(1)} %add.91), channel_id=1, source_target_pairs={{0,16},{1,17},{2,18},{3,19},{4,20},{5,21},{6,22},{7,23},{8,24},{9,... | collective-permute-start | bytes 786440 | tf_op jit(solution)/shard_map/ppermute | solution.py:10
  67.9 15.4 %collective-permute-start.5 = (f32[128,512]{0,1:T(8,128)S(1)}, f32[128,512]{0,1:T(8,128)S(1)}, u32[]{:S(2)}, u32[]{:S(2)}) collective-permute-start(f32[128,512]{0,1:T(8,128)S(1)} %add.92), channel_id=1, source_target_pairs={{0,32},{1,33},{2,34},{3,35},{4,36},{5,37},{6,38},{7,39},{8,40},{9,... | collective-permute-start | bytes 786440 | tf_op jit(solution)/shard_map/ppermute | solution.py:10
  197.9 1.2 slice-start
  224.7 0.7 copy-start.3
  251.6 0.7 copy-start.4
  345.5 2.1 copy-start.5
  351.9 10.4 %collective-permute-start.6 = (f32[512]{0:T(512)S(1)}, f32[512]{0:T(512)S(1)}, u32[]{:S(2)}, u32[]{:S(2)}) collective-permute-start(f32[512]{0:T(512)S(1)} %multiply_reduce_fusion), channel_id=1, source_target_pairs={{0,1},{1,0},{2,3},{3,2},{4,5},{5,4},{6,7},{7,6},{8,9},{9,8},{10,11... | collective-permute-start | bytes 6152 | tf_op jit(solution)/shard_map/ppermute | solution.py:10
  362.2 4.3 %collective-permute-start.7 = (f32[512]{0:T(512)S(1)}, f32[512]{0:T(512)S(1)}, u32[]{:S(2)}, u32[]{:S(2)}) collective-permute-start(f32[512]{0:T(512)S(1)} %add.95), channel_id=1, source_target_pairs={{0,2},{1,3},{2,0},{3,1},{4,6},{5,7},{6,4},{7,5},{8,10},{9,11},{10,... | collective-permute-start | bytes 6152 | tf_op jit(solution)/shard_map/ppermute | solution.py:10
  366.5 5.8 %collective-permute-start.8 = (f32[512]{0:T(512)S(1)}, f32[512]{0:T(512)S(1)}, u32[]{:S(2)}, u32[]{:S(2)}) collective-permute-start(f32[512]{0:T(512)S(1)} %add.96), channel_id=1, source_target_pairs={{0,4},{1,5},{2,6},{3,7},{4,0},{5,1},{6,2},{7,3},{8,12},{9,13},{10,... | collective-permute-start | bytes 6152 | tf_op jit(solution)/shard_map/ppermute | solution.py:10
  372.4 4.3 %collective-permute-start.9 = (f32[512]{0:T(512)S(1)}, f32[512]{0:T(512)S(1)}, u32[]{:S(2)}, u32[]{:S(2)}) collective-permute-start(f32[512]{0:T(512)S(1)} %add.97), channel_id=1, source_target_pairs={{0,8},{1,9},{2,10},{3,11},{4,12},{5,13},{6,14},{7,15},{8,0},{9,1},... | collective-permute-start | bytes 6152 | tf_op jit(solution)/shard_map/ppermute | solution.py:10
  376.7 5.2 %collective-permute-start.10 = (f32[512]{0:T(512)S(1)}, f32[512]{0:T(512)S(1)}, u32[]{:S(2)}, u32[]{:S(2)}) collective-permute-start(f32[512]{0:T(512)S(1)} %add.98), channel_id=1, source_target_pairs={{0,16},{1,17},{2,18},{3,19},{4,20},{5,21},{6,22},{7,23},{8,24},{9,... | collective-permute-start | bytes 6152 | tf_op jit(solution)/shard_map/ppermute | solution.py:10
  381.9 8.5 %collective-permute-start.11 = (f32[512]{0:T(512)S(1)}, f32[512]{0:T(512)S(1)}, u32[]{:S(2)}, u32[]{:S(2)}) collective-permute-start(f32[512]{0:T(512)S(1)} %add.99), channel_id=1, source_target_pairs={{0,32},{1,33},{2,34},{3,35},{4,36},{5,37},{6,38},{7,39},{8,40},{9,... | collective-permute-start | bytes 6152 | tf_op jit(solution)/shard_map/ppermute | solution.py:10
  390.4 1.3 copy-start.6
Sparse Core Ops, SparseCore 0:
  86.6 111.2 all-reduce.2

commit v2 on v1

--- a/solution.py
+++ b/solution.py
@@ -4,12 +4,16 @@
 from jax.sharding import PartitionSpec as P
 
 
-def xor_psum(x, axis, size):
-    step = 1
-    while step < size:
-        x = x + lax.ppermute(x, axis, [(i, i ^ step) for i in range(size)])
-        step *= 2
-    return x
+def scatter_gather_psum(x, axis, size):
+    chunks = x.reshape(size, -1, 128)
+    mine = jnp.sum(lax.all_to_all(chunks, axis, 0, 0, tiled=False), axis=0)
+    spread = jnp.broadcast_to(mine[None], chunks.shape)
+    return lax.all_to_all(spread, axis, 0, 0, tiled=False).reshape(x.shape)
+
+
+def gather_psum(x, axis, size):
+    copies = jnp.broadcast_to(x[None], (size,) + x.shape)
+    return jnp.sum(lax.all_to_all(copies, axis, 0, 0, tiled=False), axis=0)
 
 
 def local(momentum, gradient, weight, basis):
@@ -18,7 +22,7 @@
     buffer = momentum + gradient.astype(jnp.float32)
     panel_part = jnp.dot(buffer, basis, precision=highest)
     tensor_size = lax.axis_size("tensor")
-    panel_full = xor_psum(panel_part, "tensor", tensor_size)
+    panel_full = scatter_gather_psum(panel_part, "tensor", tensor_size)
     gram_part = jnp.dot(panel_full.T, panel_full, precision=highest)
     cross_part = jnp.dot(buffer.T, panel_full, precision=highest)
     merged = lax.psum(jnp.concatenate([gram_part, cross_part], axis=0), "fsdp")
@@ -31,7 +35,7 @@
     )
     orthonormal = solved[:rows]
     right_factor = solved[rows:]
-    col_sumsq = xor_psum(jnp.sum(right_factor * right_factor, axis=0), "tensor", tensor_size)
+    col_sumsq = gather_psum(jnp.sum(right_factor * right_factor, axis=0), "tensor", tensor_size)
     new_basis = right_factor / jnp.sqrt(col_sumsq + 1e-06)
     new_momentum = buffer - 0.1 * jnp.dot(orthonormal, right_factor.T, precision=highest)
     total_rows = buffer.shape[0] * lax.axis_size("fsdp")

time: 405 us -> 364 us (0.90)
  waiting for transfers between devices: 167 us -> 120 us
  blocking collectives: 0 us -> 44.7 us
  starting transfers between devices: 53.8 us -> 17.4 us
    ppermute x12 -> x0, waiting for transfers between devices: 55.5 us -> none  [xor_psum(): x = x + lax.ppermute(x, axis, [(i, i ^ step) for i in range(size)])]
    ppermute x12 -> x0, starting transfers between devices: 53.8 us -> none  [xor_psum(): x = x + lax.ppermute(x, axis, [(i, i ^ step) for i in range(size)])]
    all_to_all x0 -> x2, blocking collectives: none -> 44.7 us  [the longest x1 27 us: scatter_gather_psum(): mine = jnp.sum(lax.all_to_all(chunks, axis, 0, 0, tiled=False), axis=0)]
    all_to_all x0 -> x1, starting transfers between devices: none -> 17.3 us  [gather_psum(): return jnp.sum(lax.all_to_all(copies, axis, 0, 0, tiled=False), axis=0)]
    all_to_all x0 -> x1, waiting for transfers between devices: none -> 9.71 us  [gather_psum(): return jnp.sum(lax.all_to_all(copies, axis, 0, 0, tiled=False), axis=0)]
  transfers between devices with their start and end apart: 13 -> 2, of which waited for: 12 -> 2; matrix products, arithmetic and copies ran while one was open for 0% -> 0% of each run, Pallas kernels for 0% -> 0%
where the time goes in v2:
time: 364 us; the launch traced here: 360 us
  other arithmetic  128 us (35%)
  waiting for transfers between devices  120 us (33%)
  blocking collectives  44.7 us (12%)
  local copies, waits for them, and re-layouts  19.7 us (5%)
  starting transfers between devices  17.4 us (5%)
  between operations  17.2 us (5%)
  matrix products  13 us (4%)
    psum x1, waiting for transfers between devices, local(): merged = lax.psum(jnp.concatenate([gram_part, cross_part], axis=0), 'fsdp')  111 us
    another operation x14, other arithmetic, local(): factor = jnp.linalg.cholesky(gram_matrix)  84.8 us
    another operation x3, other arithmetic, local(): lax.linalg.triangular_solve(factor, jnp.concatenate([panel_full, cross],...  40.3 us
    all_to_all x1, blocking collectives, scatter_gather_psum(): mine = jnp.sum(lax.all_to_all(chunks, axis, 0, 0, tiled=False), axis=0)  27 us
    all_to_all x1, blocking collectives, scatter_gather_psum(): return lax.all_to_all(spread, axis, 0, 0, tiled=False).reshape(x.shape)  17.7 us
    all_to_all x1, starting transfers between devices, gather_psum(): return jnp.sum(lax.all_to_all(copies, axis, 0, 0, tiled=False), axis=0)  17.3 us
    another operation x12, local copies, waits for them, and re-layouts  10.4 us
    all_to_all x1, waiting for transfers between devices, gather_psum(): return jnp.sum(lax.all_to_all(copies, axis, 0, 0, tiled=False), axis=0)  9.71 us
  transfers between devices with their start and end apart: 2, of which 2 were waited for; matrix products, arithmetic and copies ran while one was open for 0% of the time, Pallas kernels for 0%

profile of v2, /device:TPU:1, one launch (start us, length us, event | category | flops | bytes accessed | tf_op | source)
XLA Modules:
  0.0 360.5 jit_solution(15692873246943398653)
XLA Ops:
  7.2 1.1 copy-done
  8.3 1.6 fusion.26
  10.0 27.0 %all_to_all.16 = f32[64,8,128]{2,1,0:T(8,128)S(1)} all-to-all(f32[64,8,128]{2,1,0:T(8,128)S(1)} %reshape.58), channel_id=1, replica_groups=mesh['fsdp'=12,'tensor'=64] {'tensor'}, dimensions={0} | all-to-all | bytes 524288 | tf_op jit(solution)/shard_map/all_to_all | solution.py:9
  37.1 17.7 %all_to_all.17 = f32[64,8,128]{2,1,0:T(8,128)S(1)} all-to-all(f32[64,8,128]{2,1,0:T(8,128)S(1)} %broadcast_in_dim.6), channel_id=1, replica_groups=mesh['fsdp'=12,'tensor'=64] {'tensor'}, dimensions={0} | all-to-all | bytes 524288 | tf_op jit(solution)/shard_map/all_to_all | solution.py:11
  54.8 0.8 fusion.25
  55.7 1.0 fusion.40
  56.7 1.3 pad_maximum_fusion
  58.2 110.5 %all-reduce.3.cloned.1.call-done = f32[896,512]{0,1:T(8,128)} async-done(((f32[896,512]{0,1:T(8,128)}), f32[896,512]{0,1:T(8,128)}) %all-reduce.3.cloned.1.call-update) | async-done | bytes 1835024 | tf_op jit(solution)/shard_map/psum | solution.py:28
  168.7 1.2 slice-done
  170.3 1.4 fusion.3
  171.8 11.7 %cholesky.104 = f32[128,128]{1,0:T(8,128)S(1)} custom-call(f32[128,128]{1,0:T(8,128)S(1)} %cholesky.266), custom_call_target="Cholesky" | custom-call | tf_op jit(solution)/shard_map/jit(cholesky)/cholesky | solution.py:31
  184.3 10.6 %custom-call.30 = f32[1,128,128]{1,2,0:T(8,128)S(1)} custom-call(f32[1,128,128]{2,1,0:T(8,128)} %get-tuple-element.42), custom_call_target="InvertDiagBlocksLowerTriangular" | custom-call | tf_op jit(solution)/shard_map/jit(cholesky)/cholesky | solution.py:31
  196.9 12.7 %cholesky.217 = f32[128,128]{1,0:T(8,128)S(1)} custom-call(f32[128,128]{1,0:T(8,128)} %cholesky.270), custom_call_target="Cholesky" | custom-call | tf_op jit(solution)/shard_map/jit(cholesky)/cholesky | solution.py:31
  210.2 10.6 %custom-call.31 = f32[1,128,128]{1,2,0:T(8,128)S(1)} custom-call(f32[1,128,128]{2,1,0:T(8,128)} %get-tuple-element.39), custom_call_target="InvertDiagBlocksLowerTriangular" | custom-call | tf_op jit(solution)/shard_map/jit(cholesky)/cholesky | solution.py:31
  220.9 1.2 convolution_dynamic-update-slice_fusion
  223.7 12.5 %cholesky.238 = f32[128,128]{1,0:T(8,128)S(1)} custom-call(f32[128,128]{1,0:T(8,128)} %cholesky.275), custom_call_target="Cholesky" | custom-call | tf_op jit(solution)/shard_map/jit(cholesky)/cholesky | solution.py:31
  236.9 10.6 %custom-call.32 = f32[1,128,128]{1,2,0:T(8,128)S(1)} custom-call(f32[1,128,128]{2,1,0:T(8,128)} %get-tuple-element.36), custom_call_target="InvertDiagBlocksLowerTriangular" | custom-call | tf_op jit(solution)/shard_map/jit(cholesky)/cholesky | solution.py:31
  247.6 1.0 convolution_dynamic-update-slice_fusion.1
  249.0 11.9 %cholesky.255 = f32[128,128]{1,0:T(8,128)S(1)} custom-call(f32[128,128]{1,0:T(8,128)S(1)} %convolution_subtract_fusion.5), custom_call_target="Cholesky" | custom-call | tf_op jit(solution)/shard_map/jit(cholesky)/cholesky | solution.py:31
  265.7 10.5 %while.1 = (s32[]{:T(128)}, f32[512,512]{1,0:T(8,128)S(1)}, s32[4,2]{0,1:T(2,128)S(1)}, f32[4,128,128]{2,1,0:T(8,128)}, s32[]{:T(128)}) while((s32[]{:T(128)}, f32[512,512]{1,0:T(8,128)S(1)}, s32[4,2]{0,1:T(2,128)S(1)}, f32[4,128,128]{2,1,0:T(8,128)}, s32[]{:T(128)}) %tuple.35), condition=%wide.while_cond, body=%wide.while_body.sunk | while | flops 2 | bytes 132205 | solution.py:33
  266.3 2.0 bitcast_dynamic-update-slice_fusion.2
  268.9 2.0 bitcast_dynamic-update-slice_fusion.2
  271.5 2.0 bitcast_dynamic-update-slice_fusion.2
  274.1 2.0 bitcast_dynamic-update-slice_fusion.2
  276.1 40.1 %custom-call.33 = f32[4,128,128]{1,2,0:T(8,128)S(1)} custom-call(f32[4,128,128]{2,1,0:T(8,128)} %get-tuple-element.10), custom_call_target="InvertDiagBlocksLowerTriangular" | custom-call | tf_op jit(solution)/shard_map/triangular_solve | solution.py:33
  316.3 1.3 slice.130
  321.4 0.7 broadcast_in_dim.7
  322.2 17.3 %all-to-all-start.2 = ((f32[64,1,512]{2,1,0:T(1,128)}), f32[64,1,512]{2,1,0:T(1,128)S(1)}, u32[]{:S(2)}, u32[]{:S(2)}) async-start(f32[64,1,512]{2,1,0:T(1,128)} %broadcast_in_dim.7), calls=%async_computation.2 | async-start | bytes 262144 | tf_op jit(solution)/shard_map/all_to_all | solution.py:16
  339.5 1.4 fusion
  340.9 9.7 %all-to-all-done.2 = f32[64,1,512]{2,1,0:T(1,128)S(1)} async-done(((f32[64,1,512]{2,1,0:T(1,128)}), f32[64,1,512]{2,1,0:T(1,128)S(1)}, u32[]{:S(2)}, u32[]{:S(2)}) %all-to-all-start.2) | async-done | bytes 131104 | tf_op jit(solution)/shard_map/all_to_all | solution.py:16
  350.9 1.1 copy.32
  352.1 1.4 fusion.2
  (62 shorter events, 15.3 us)
Async XLA Ops:
  7.2 1.1 copy-start
  7.2 47.6 %copy-start.1 = (f32[128,384]{1,0:T(8,128)S(1)}, f32[128,384]{1,0:T(8,128)}, u32[]{:S(2)}) copy-start(f32[128,384]{1,0:T(8,128)} %param.4) | copy-start | bytes 589828
  7.2 47.6 %copy-start.2 = (bf16[128,384]{1,0:T(8,128)(2,1)S(1)}, bf16[128,384]{1,0:T(8,128)(2,1)}, u32[]{:S(2)}) copy-start(bf16[128,384]{1,0:T(8,128)(2,1)} %param.5) | copy-start | bytes 294916
  7.2 161.5 %all-reduce.3.cloned.1.call-start = ((), (), s32[]{:S(2)}) async-start(), calls=%async_computation.3 | async-start | bytes 3670016 | tf_op jit(solution)/shard_map/psum | solution.py:28
  168.7 1.2 slice-start
  195.6 0.7 copy-start.3
  222.5 0.7 copy-start.4
  316.3 2.1 copy-start.5
  318.8 1.0 copy-start.6
  322.2 28.5 %all-to-all-start.2 = ((f32[64,1,512]{2,1,0:T(1,128)}), f32[64,1,512]{2,1,0:T(1,128)S(1)}, u32[]{:S(2)}, u32[]{:S(2)}) async-start(f32[64,1,512]{2,1,0:T(1,128)} %broadcast_in_dim.7), calls=%async_computation.2 | async-start | bytes 262144 | tf_op jit(solution)/shard_map/all_to_all | solution.py:16
  340.9 11.1 %copy-start.7 = (bf16[128,384]{1,0:T(8,128)(2,1)S(1)}, bf16[128,384]{1,0:T(8,128)(2,1)}, u32[]{:S(2)}) copy-start(bf16[128,384]{1,0:T(8,128)(2,1)} %param.6) | copy-start | bytes 294916
Sparse Core Ops, SparseCore 0:
  58.2 110.5 all-reduce.2

commit v3 on v2

--- a/solution.py
+++ b/solution.py
@@ -9,6 +9,32 @@
     mine = jnp.sum(lax.all_to_all(chunks, axis, 0, 0, tiled=False), axis=0)
     spread = jnp.broadcast_to(mine[None], chunks.shape)
     return lax.all_to_all(spread, axis, 0, 0, tiled=False).reshape(x.shape)
+
+
+def padded_scatter_gather_psum(x, axis, size):
+    flat = x.reshape(-1)
+    chunk = size * 8 * 128
+    padded = jnp.pad(flat, (0, (-flat.shape[0]) % chunk))
+    summed = scatter_gather_psum(padded.reshape(-1, 128), axis, size)
+    return summed.reshape(-1)[: flat.shape[0]].reshape(x.shape)
+
+
+def lower_blocks(matrix, block):
+    count = matrix.shape[0] // block
+    return jnp.stack([matrix[i * block:(i + 1) * block, j * block:(j + 1) * block] for i in range(count) for j in range(i + 1)])
+
+
+def symmetric_from_lower_blocks(blocks, count):
+    block = blocks.shape[-1]
+    index = {}
+    for i in range(count):
+        for j in range(i + 1):
+            index[(i, j)] = len(index)
+    rows = []
+    for i in range(count):
+        row = [blocks[index[(i, j)]] if j <= i else blocks[index[(j, i)]].T for j in range(count)]
+        rows.append(jnp.concatenate(row, axis=1))
+    return jnp.concatenate(rows, axis=0)
 
 
 def gather_psum(x, axis, size):
@@ -24,10 +50,11 @@
     tensor_size = lax.axis_size("tensor")
     panel_full = scatter_gather_psum(panel_part, "tensor", tensor_size)
     gram_part = jnp.dot(panel_full.T, panel_full, precision=highest)
-    cross_part = jnp.dot(buffer.T, panel_full, precision=highest)
-    merged = lax.psum(jnp.concatenate([gram_part, cross_part], axis=0), "fsdp")
-    gram_matrix = merged[:rank]
-    cross = merged[rank:]
+    block = 128
+    fsdp_size = lax.axis_size("fsdp")
+    gram_blocks = padded_scatter_gather_psum(lower_blocks(gram_part, block), "fsdp", fsdp_size)
+    cross = padded_scatter_gather_psum(jnp.dot(buffer.T, panel_full, precision=highest), "fsdp", fsdp_size)
+    gram_matrix = symmetric_from_lower_blocks(gram_blocks, rank // block)
     factor = jnp.linalg.cholesky(gram_matrix)
     rows = panel_full.shape[0]
     solved = lax.linalg.triangular_solve(

time: 364 us -> 339 us (0.931)
  waiting for transfers between devices: 120 us -> 86.4 us
  starting transfers between devices: 17.4 us -> 39.9 us
  between operations: 17.2 us -> 4.09 us
  other arithmetic: 128 us -> 121 us
    psum x1 -> x0, waiting for transfers between devices: 111 us -> none  [local(): merged = lax.psum(jnp.concatenate([gram_part, cross_part], axis=0), 'fsdp')]
    all_to_all x0 -> x4, waiting for transfers between devices: none -> 76.7 us  [the longest x2 51.9 us: scatter_gather_psum(): mine = jnp.sum(lax.all_to_all(chunks, axis, 0, 0, tiled=False), axis=0)]
    all_to_all x0 -> x4, starting transfers between devices: none -> 34.5 us  [the longest x2 19.4 us: scatter_gather_psum(): mine = jnp.sum(lax.all_to_all(chunks, axis, 0, 0, tiled=False), axis=0)]
    all_to_all x1, starting transfers between devices: 17.3 us -> 5.41 us  [gather_psum(): return jnp.sum(lax.all_to_all(copies, axis, 0, 0, tiled=False), axis=0)]
    another operation x14 -> x15, other arithmetic: 84.8 us -> 79.2 us  [local(): factor = jnp.linalg.cholesky(gram_matrix)]
    another operation x12 -> x15, local copies, waits for them, and re-layouts: 10.4 us -> 12.6 us
  transfers between devices with their start and end apart: 2 -> 5, of which waited for: 2 -> 4; matrix products, arithmetic and copies ran while one was open for 0% -> 42% of each run, Pallas kernels for 0% -> 0%
where the time goes in v3:
time: 339 us; the launch traced here: 333 us
  other arithmetic  121 us (36%)
  waiting for transfers between devices  86.4 us (25%)
  blocking collectives  44.7 us (13%)
  starting transfers between devices  39.9 us (12%)
  local copies, waits for them, and re-layouts  22.3 us (7%)
  matrix products  14.8 us (4%)
  between operations  4.09 us (1%)
    another operation x15, other arithmetic, local(): factor = jnp.linalg.cholesky(gram_matrix)  79.2 us
    all_to_all x2, waiting for transfers between devices, scatter_gather_psum(): mine = jnp.sum(lax.all_to_all(chunks, axis, 0, 0, tiled=False), axis=0)  51.9 us
    another operation x3, other arithmetic, local(): lax.linalg.triangular_solve(factor, jnp.concatenate([panel_full, cross],...  40.3 us
    all_to_all x1, blocking collectives, scatter_gather_psum(): mine = jnp.sum(lax.all_to_all(chunks, axis, 0, 0, tiled=False), axis=0)  27 us
    all_to_all x2, waiting for transfers between devices, scatter_gather_psum(): return lax.all_to_all(spread, axis, 0, 0, tiled=False).reshape(x.shape)  24.8 us
    all_to_all x2, starting transfers between devices, scatter_gather_psum(): mine = jnp.sum(lax.all_to_all(chunks, axis, 0, 0, tiled=False), axis=0)  19.4 us
    all_to_all x1, blocking collectives, scatter_gather_psum(): return lax.all_to_all(spread, axis, 0, 0, tiled=False).reshape(x.shape)  17.7 us
    all_to_all x2, starting transfers between devices, scatter_gather_psum(): return lax.all_to_all(spread, axis, 0, 0, tiled=False).reshape(x.shape)  15 us
  transfers between devices with their start and end apart: 5, of which 4 were waited for; matrix products, arithmetic and copies ran while one was open for 42% of the time, Pallas kernels for 0%

profile of v3, /device:TPU:1, one launch (start us, length us, event | category | flops | bytes accessed | tf_op | source)
XLA Modules:
  0.0 333.5 jit_solution(6452980200414304516)
XLA Ops:
  1.8 1.6 fusion.23
  3.4 27.0 %all_to_all.36 = f32[64,8,128]{2,1,0:T(8,128)S(1)} all-to-all(f32[64,8,128]{2,1,0:T(8,128)S(1)} %reshape.110), channel_id=1, replica_groups=mesh['fsdp'=12,'tensor'=64] {'tensor'}, dimensions={0} | all-to-all | bytes 524288 | tf_op jit(solution)/shard_map/all_to_all | solution.py:9
  30.5 17.7 %all_to_all.37 = f32[64,8,128]{2,1,0:T(8,128)S(1)} all-to-all(f32[64,8,128]{2,1,0:T(8,128)S(1)} %broadcast_in_dim.9), channel_id=1, replica_groups=mesh['fsdp'=12,'tensor'=64] {'tensor'}, dimensions={0} | all-to-all | bytes 524288 | tf_op jit(solution)/shard_map/all_to_all | solution.py:11
  50.4 12.6 %all-to-all-start.4 = ((f32[12,112,128]{2,1,0:T(8,128)}), f32[12,112,128]{2,1,0:T(8,128)S(1)}, u32[]{:S(2)}, u32[]{:S(2)}) async-start(f32[12,112,128]{2,1,0:T(8,128)} %bitcast.11), calls=%async_computation.4 | async-start | bytes 1376256 | tf_op jit(solution)/shard_map/all_to_all | solution.py:9
  64.8 23.9 %all-to-all-done.4 = f32[12,112,128]{2,1,0:T(8,128)S(1)} async-done(((f32[12,112,128]{2,1,0:T(8,128)}), f32[12,112,128]{2,1,0:T(8,128)S(1)}, u32[]{:S(2)}, u32[]{:S(2)}) %all-to-all-start.4) | async-done | bytes 688160 | tf_op jit(solution)/shard_map/all_to_all | solution.py:9
  88.6 6.9 %all-to-all-start.2 = ((f32[12,128,128]{2,1,0:T(8,128)}), f32[12,128,128]{2,1,0:T(8,128)S(1)}, u32[]{:S(2)}, u32[]{:S(2)}) async-start(f32[12,128,128]{2,1,0:T(8,128)} %reshape_reshape.7), calls=%async_computation.2 | async-start | bytes 1572864 | tf_op jit(solution)/shard_map/all_to_all | solution.py:9
  95.5 28.0 %all-to-all-done.2 = f32[12,128,128]{2,1,0:T(8,128)S(1)} async-done(((f32[12,128,128]{2,1,0:T(8,128)}), f32[12,128,128]{2,1,0:T(8,128)S(1)}, u32[]{:S(2)}, u32[]{:S(2)}) %all-to-all-start.2) | async-done | bytes 786464 | tf_op jit(solution)/shard_map/all_to_all | solution.py:9
  124.5 7.6 %all-to-all-start.5 = ((f32[12,112,128]{2,1,0:T(8,128)}), f32[12,112,128]{2,1,0:T(8,128)S(1)}, u32[]{:S(2)}, u32[]{:S(2)}) async-start(f32[12,112,128]{2,1,0:T(8,128)} %broadcast_in_dim.11), calls=%async_computation.5 | async-start | bytes 1376256 | tf_op jit(solution)/shard_map/all_to_all | solution.py:11
  132.9 24.8 %all-to-all-done.5 = f32[12,112,128]{2,1,0:T(8,128)S(1)} async-done(((f32[12,112,128]{2,1,0:T(8,128)}), f32[12,112,128]{2,1,0:T(8,128)S(1)}, u32[]{:S(2)}, u32[]{:S(2)}) %all-to-all-start.5) | async-done | bytes 688160 | tf_op jit(solution)/shard_map/all_to_all | solution.py:11
  158.6 7.5 %all-to-all-start.3 = ((f32[12,128,128]{2,1,0:T(8,128)}), f32[12,128,128]{2,1,0:T(8,128)}, u32[]{:S(2)}, u32[]{:S(2)}) async-start(f32[12,128,128]{2,1,0:T(8,128)} %broadcast_in_dim.10), calls=%async_computation.3 | async-start | bytes 1572864 | tf_op jit(solution)/shard_map/all_to_all | solution.py:11
  168.2 1.2 fusion.3
  169.4 11.7 %cholesky.104 = f32[128,128]{1,0:T(8,128)S(1)} custom-call(f32[128,128]{1,0:T(8,128)S(1)} %cholesky.266), custom_call_target="Cholesky" | custom-call | tf_op jit(solution)/shard_map/jit(cholesky)/cholesky | solution.py:58
  181.3 9.8 %custom-call.30 = f32[1,128,128]{1,2,0:T(8,128)S(1)} custom-call(f32[1,128,128]{2,1,0:T(8,128)S(1)} %get-tuple-element.54), custom_call_target="InvertDiagBlocksLowerTriangular" | custom-call | tf_op jit(solution)/shard_map/jit(cholesky)/cholesky | solution.py:58
  191.8 11.7 %cholesky.217 = f32[128,128]{1,0:T(8,128)S(1)} custom-call(f32[128,128]{1,0:T(8,128)S(1)} %cholesky.270), custom_call_target="Cholesky" | custom-call | tf_op jit(solution)/shard_map/jit(cholesky)/cholesky | solution.py:58
  204.1 9.9 %custom-call.31 = f32[1,128,128]{1,2,0:T(8,128)S(1)} custom-call(f32[1,128,128]{2,1,0:T(8,128)S(1)} %get-tuple-element.51), custom_call_target="InvertDiagBlocksLowerTriangular" | custom-call | tf_op jit(solution)/shard_map/jit(cholesky)/cholesky | solution.py:58
  214.8 11.7 %cholesky.238 = f32[128,128]{1,0:T(8,128)S(1)} custom-call(f32[128,128]{1,0:T(8,128)S(1)} %cholesky.275), custom_call_target="Cholesky" | custom-call | tf_op jit(solution)/shard_map/jit(cholesky)/cholesky | solution.py:58
  226.5 9.8 %custom-call.32 = f32[1,128,128]{1,2,0:T(8,128)S(1)} custom-call(f32[1,128,128]{2,1,0:T(8,128)S(1)} %get-tuple-element.48), custom_call_target="InvertDiagBlocksLowerTriangular" | custom-call | tf_op jit(solution)/shard_map/jit(cholesky)/cholesky | solution.py:58
  236.9 11.8 %cholesky.255 = f32[128,128]{1,0:T(8,128)S(1)} custom-call(f32[128,128]{1,0:T(8,128)S(1)} %convolution_subtract_fusion.5), custom_call_target="Cholesky" | custom-call | tf_op jit(solution)/shard_map/jit(cholesky)/cholesky | solution.py:58
  253.5 10.4 %while.1 = (s32[]{:T(128)}, f32[512,512]{1,0:T(8,128)S(1)}, s32[4,2]{0,1:T(2,128)S(1)}, f32[4,128,128]{2,1,0:T(8,128)}, s32[]{:T(128)}) while((s32[]{:T(128)}, f32[512,512]{1,0:T(8,128)S(1)}, s32[4,2]{0,1:T(2,128)S(1)}, f32[4,128,128]{2,1,0:T(8,128)}, s32[]{:T(128)}) %tuple.46), condition=%wide.while_cond, body=%wide.while_body.sunk | while | flops 2 | bytes 132705 | solution.py:60
  254.1 2.0 bitcast_dynamic-update-slice_fusion.2
  256.7 2.0 bitcast_dynamic-update-slice_fusion.2
  259.3 2.0 bitcast_dynamic-update-slice_fusion.2
  261.9 2.0 bitcast_dynamic-update-slice_fusion.2
  263.9 40.1 %custom-call.33 = f32[4,128,128]{1,2,0:T(8,128)S(1)} custom-call(f32[4,128,128]{2,1,0:T(8,128)} %get-tuple-element.10), custom_call_target="InvertDiagBlocksLowerTriangular" | custom-call | tf_op jit(solution)/shard_map/triangular_solve | solution.py:60
  304.0 1.3 reshape_reshape_reshape.3
  306.3 1.5 fusion.13
  307.7 1.5 convolution_subtract_fusion.1
  311.1 1.5 convolution_subtract_fusion.2
  313.9 5.4 %all-to-all-start.6 = ((f32[64,1,512]{2,1,0:T(1,128)}), f32[64,1,512]{2,1,0:T(1,128)S(1)}, u32[]{:S(2)}, u32[]{:S(2)}) async-start(f32[64,1,512]{2,1,0:T(1,128)} %broadcast_in_dim.12), calls=%async_computation.6 | async-start | bytes 262144 | tf_op jit(solution)/shard_map/all_to_all | solution.py:42
  319.3 1.4 fusion
  320.7 9.7 %all-to-all-done.6 = f32[64,1,512]{2,1,0:T(1,128)S(1)} async-done(((f32[64,1,512]{2,1,0:T(1,128)}), f32[64,1,512]{2,1,0:T(1,128)S(1)}, u32[]{:S(2)}, u32[]{:S(2)}) %all-to-all-start.6) | async-done | bytes 131104 | tf_op jit(solution)/shard_map/all_to_all | solution.py:42
  331.9 1.4 fusion.2
  (104 shorter events, 22.4 us)
Async XLA Ops:
  0.6 1.1 copy-start
  50.4 12.6 %copy-start.1 = (f32[128,384]{1,0:T(8,128)S(1)}, f32[128,384]{1,0:T(8,128)}, u32[]{:S(2)}) copy-start(f32[128,384]{1,0:T(8,128)} %param.4) | copy-start | bytes 589828
  50.4 12.6 %copy-start.5 = (bf16[128,384]{1,0:T(8,128)(2,1)S(1)}, bf16[128,384]{1,0:T(8,128)(2,1)}, u32[]{:S(2)}) copy-start(bf16[128,384]{1,0:T(8,128)(2,1)} %param.5) | copy-start | bytes 294916
  50.4 38.2 %all-to-all-start.4 = ((f32[12,112,128]{2,1,0:T(8,128)}), f32[12,112,128]{2,1,0:T(8,128)S(1)}, u32[]{:S(2)}, u32[]{:S(2)}) async-start(f32[12,112,128]{2,1,0:T(8,128)} %bitcast.11), calls=%async_computation.4 | async-start | bytes 1376256 | tf_op jit(solution)/shard_map/all_to_all | solution.py:9
  88.6 35.0 %all-to-all-start.2 = ((f32[12,128,128]{2,1,0:T(8,128)}), f32[12,128,128]{2,1,0:T(8,128)S(1)}, u32[]{:S(2)}, u32[]{:S(2)}) async-start(f32[12,128,128]{2,1,0:T(8,128)} %reshape_reshape.7), calls=%async_computation.2 | async-start | bytes 1572864 | tf_op jit(solution)/shard_map/all_to_all | solution.py:9
  124.5 33.2 %all-to-all-start.5 = ((f32[12,112,128]{2,1,0:T(8,128)}), f32[12,112,128]{2,1,0:T(8,128)S(1)}, u32[]{:S(2)}, u32[]{:S(2)}) async-start(f32[12,112,128]{2,1,0:T(8,128)} %broadcast_in_dim.11), calls=%async_computation.5 | async-start | bytes 1376256 | tf_op jit(solution)/shard_map/all_to_all | solution.py:11
  158.6 145.5 %all-to-all-start.3 = ((f32[12,128,128]{2,1,0:T(8,128)}), f32[12,128,128]{2,1,0:T(8,128)}, u32[]{:S(2)}, u32[]{:S(2)}) async-start(f32[12,128,128]{2,1,0:T(8,128)} %broadcast_in_dim.10), calls=%async_computation.3 | async-start | bytes 1572864 | tf_op jit(solution)/shard_map/all_to_all | solution.py:11
  166.1 1.1 copy-start.7
  166.1 1.1 copy-start.8
  166.4 0.8 copy-start.4
  167.0 0.6 copy-start.9
  167.1 0.6 copy-start.10
  167.2 0.6 copy-start.11
  306.3 3.4 %copy-start.3 = (f32[512,512]{1,0:T(8,128)S(1)}, f32[512,512]{1,0:T(8,128)}, u32[]{:S(2)}) copy-start(f32[512,512]{1,0:T(8,128)} %constant_dynamic-update-slice_fusion) | copy-start | bytes 3145732
  313.2 6.2 %copy-start.2 = (f32[128,384]{1,0:T(8,128)S(1)}, f32[128,384]{1,0:T(8,128)}, u32[]{:S(2)}) copy-start(f32[128,384]{1,0:T(8,128)} %param.4) | copy-start | bytes 589828
  313.9 5.4 %copy-start.6 = (bf16[128,384]{1,0:T(8,128)(2,1)S(1)}, bf16[128,384]{1,0:T(8,128)(2,1)}, u32[]{:S(2)}) copy-start(bf16[128,384]{1,0:T(8,128)(2,1)} %param.5) | copy-start | bytes 294916
  313.9 16.5 %all-to-all-start.6 = ((f32[64,1,512]{2,1,0:T(1,128)}), f32[64,1,512]{2,1,0:T(1,128)S(1)}, u32[]{:S(2)}, u32[]{:S(2)}) async-start(f32[64,1,512]{2,1,0:T(1,128)} %broadcast_in_dim.12), calls=%async_computation.6 | async-start | bytes 262144 | tf_op jit(solution)/shard_map/all_to_all | solution.py:42
  330.7 1.2 copy-start.12

commit v4 on v3

--- a/solution.py
+++ b/solution.py
@@ -53,7 +53,10 @@
     block = 128
     fsdp_size = lax.axis_size("fsdp")
     gram_blocks = padded_scatter_gather_psum(lower_blocks(gram_part, block), "fsdp", fsdp_size)
-    cross = padded_scatter_gather_psum(jnp.dot(buffer.T, panel_full, precision=highest), "fsdp", fsdp_size)
+    cross_part, gram_blocks = lax.optimization_barrier(
+        (jnp.dot(buffer.T, panel_full, precision=highest), gram_blocks)
+    )
+    cross = padded_scatter_gather_psum(cross_part, "fsdp", fsdp_size)
     gram_matrix = symmetric_from_lower_blocks(gram_blocks, rank // block)
     factor = jnp.linalg.cholesky(gram_matrix)
     rows = panel_full.shape[0]

time: 339 us -> 326 us (0.962)
  waiting for transfers between devices: 86.4 us -> 33 us
  blocking collectives: 44.7 us -> 84.9 us
  starting transfers between devices: 39.9 us -> 27 us
  matrix products: 14.8 us -> 21.2 us
  local copies, waits for them, and re-layouts: 22.3 us -> 27.7 us
    all_to_all x2 -> x1, waiting for transfers between devices: 51.9 us -> 0.01 us  [scatter_gather_psum(): mine = jnp.sum(lax.all_to_all(chunks, axis, 0, 0, tiled=False), axis=0)]
    all_to_all x1 -> x2, blocking collectives: 27 us -> 67.2 us  [scatter_gather_psum(): mine = jnp.sum(lax.all_to_all(chunks, axis, 0, 0, tiled=False), axis=0)]
    all_to_all x2 -> x1, starting transfers between devices: 19.4 us -> 6.96 us  [scatter_gather_psum(): mine = jnp.sum(lax.all_to_all(chunks, axis, 0, 0, tiled=False), axis=0)]
    another operation x6, matrix products: 1.87 us -> 5.47 us  [local(): factor = jnp.linalg.cholesky(gram_matrix)]
    another operation x12, local copies, waits for them, and re-layouts: 10.4 us -> 14 us
  transfers between devices with their start and end apart: 5 -> 4, of which waited for: 4 -> 2; matrix products, arithmetic and copies ran while one was open for 42% -> 45% of each run, Pallas kernels for 0% -> 0%
where the time goes in v4:
time: 326 us; the launch traced here: 320 us
  other arithmetic  122 us (37%)
  blocking collectives  84.9 us (26%)
  waiting for transfers between devices  33 us (10%)
  local copies, waits for them, and re-layouts  27.7 us (8%)
  starting transfers between devices  27 us (8%)
  matrix products  21.2 us (7%)
  between operations  4.05 us (1%)
    another operation x15, other arithmetic, local(): factor = jnp.linalg.cholesky(gram_matrix)  79.1 us
    all_to_all x2, blocking collectives, scatter_gather_psum(): mine = jnp.sum(lax.all_to_all(chunks, axis, 0, 0, tiled=False), axis=0)  67.2 us
    another operation x3, other arithmetic, local(): lax.linalg.triangular_solve(factor, jnp.concatenate([panel_full, cross],...  41.3 us
    all_to_all x2, waiting for transfers between devices, scatter_gather_psum(): return lax.all_to_all(spread, axis, 0, 0, tiled=False).reshape(x.shape)  23.3 us
    all_to_all x1, blocking collectives, scatter_gather_psum(): return lax.all_to_all(spread, axis, 0, 0, tiled=False).reshape(x.shape)  17.7 us
    another operation x12, local copies, waits for them, and re-layouts  14 us
    all_to_all x2, starting transfers between devices, scatter_gather_psum(): return lax.all_to_all(spread, axis, 0, 0, tiled=False).reshape(x.shape)  13.6 us
    all_to_all x1, waiting for transfers between devices, gather_psum(): return jnp.sum(lax.all_to_all(copies, axis, 0, 0, tiled=False), axis=0)  9.71 us
  transfers between devices with their start and end apart: 4, of which 2 were waited for; matrix products, arithmetic and copies ran while one was open for 45% of the time, Pallas kernels for 0%

profile of v4, /device:TPU:1, one launch (start us, length us, event | category | flops | bytes accessed | tf_op | source)
XLA Modules:
  0.0 320.0 jit_solution(12977167281135365538)
XLA Ops:
  1.8 1.6 fusion.23
  3.4 27.0 %all_to_all.36 = f32[64,8,128]{2,1,0:T(8,128)S(1)} all-to-all(f32[64,8,128]{2,1,0:T(8,128)S(1)} %reshape.68), channel_id=1, replica_groups=mesh['fsdp'=12,'tensor'=64] {'tensor'}, dimensions={0} | all-to-all | bytes 524288 | tf_op jit(solution)/shard_map/all_to_all | solution.py:9
  30.5 17.7 %all_to_all.37 = f32[64,8,128]{2,1,0:T(8,128)S(1)} all-to-all(f32[64,8,128]{2,1,0:T(8,128)S(1)} %broadcast_in_dim.9), channel_id=1, replica_groups=mesh['fsdp'=12,'tensor'=64] {'tensor'}, dimensions={0} | all-to-all | bytes 524288 | tf_op jit(solution)/shard_map/all_to_all | solution.py:11
  49.6 40.2 %all_to_all.38 = f32[12,112,128]{2,1,0:T(8,128)S(1)} all-to-all(f32[12,112,128]{2,1,0:T(8,128)S(1)} %bitcast.137), channel_id=1, replica_groups=mesh['fsdp'=12,'tensor'=64] {'fsdp'}, dimensions={0} | all-to-all | bytes 1376256 | tf_op jit(solution)/shard_map/all_to_all | solution.py:9
  90.7 4.4 %all-to-all-start.3 = ((f32[12,112,128]{2,1,0:T(8,128)}), f32[12,112,128]{2,1,0:T(8,128)S(1)}, u32[]{:S(2)}, u32[]{:S(2)}) async-start(f32[12,112,128]{2,1,0:T(8,128)} %broadcast_in_dim.10), calls=%async_computation.3 | async-start | bytes 1376256 | tf_op jit(solution)/shard_map/all_to_all | solution.py:11
  96.2 1.7 fusion.22
  97.9 23.3 %all-to-all-done.3 = f32[12,112,128]{2,1,0:T(8,128)S(1)} async-done(((f32[12,112,128]{2,1,0:T(8,128)}), f32[12,112,128]{2,1,0:T(8,128)S(1)}, u32[]{:S(2)}, u32[]{:S(2)}) %all-to-all-start.3) | async-done | bytes 688160 | tf_op jit(solution)/shard_map/all_to_all | solution.py:11
  124.6 2.1 reshape_reshape.11
  126.7 7.0 %all-to-all-start.4 = ((f32[12,128,128]{2,1,0:T(8,128)}), f32[12,128,128]{2,1,0:T(8,128)S(1)}, u32[]{:S(2)}, u32[]{:S(2)}) async-start(f32[12,128,128]{2,1,0:T(8,128)} %reshape_reshape.11), calls=%async_computation.4 | async-start | bytes 1572864 | tf_op jit(solution)/shard_map/all_to_all | solution.py:9
  135.9 11.7 %cholesky.104 = f32[128,128]{1,0:T(8,128)S(1)} custom-call(f32[128,128]{1,0:T(8,128)S(1)} %cholesky.266), custom_call_target="Cholesky" | custom-call | tf_op jit(solution)/shard_map/jit(cholesky)/cholesky | solution.py:61
  147.7 9.8 %custom-call.30 = f32[1,128,128]{1,2,0:T(8,128)S(1)} custom-call(f32[1,128,128]{2,1,0:T(8,128)S(1)} %get-tuple-element.62), custom_call_target="InvertDiagBlocksLowerTriangular" | custom-call | tf_op jit(solution)/shard_map/jit(cholesky)/cholesky | solution.py:61
  160.1 11.7 %cholesky.217 = f32[128,128]{1,0:T(8,128)S(1)} custom-call(f32[128,128]{1,0:T(8,128)S(1)} %cholesky.270), custom_call_target="Cholesky" | custom-call | tf_op jit(solution)/shard_map/jit(cholesky)/cholesky | solution.py:61
  171.8 10.0 %custom-call.31 = f32[1,128,128]{1,2,0:T(8,128)S(1)} custom-call(f32[1,128,128]{2,1,0:T(8,128)S(1)} %get-tuple-element.59), custom_call_target="InvertDiagBlocksLowerTriangular" | custom-call | tf_op jit(solution)/shard_map/jit(cholesky)/cholesky | solution.py:61
  182.1 1.3 convolution_subtract_fusion.4
  183.4 11.7 %cholesky.238 = f32[128,128]{1,0:T(8,128)S(1)} custom-call(f32[128,128]{1,0:T(8,128)S(1)} %cholesky.275), custom_call_target="Cholesky" | custom-call | tf_op jit(solution)/shard_map/jit(cholesky)/cholesky | solution.py:61
  195.1 9.8 %custom-call.32 = f32[1,128,128]{1,2,0:T(8,128)S(1)} custom-call(f32[1,128,128]{2,1,0:T(8,128)S(1)} %get-tuple-element.56), custom_call_target="InvertDiagBlocksLowerTriangular" | custom-call | tf_op jit(solution)/shard_map/jit(cholesky)/cholesky | solution.py:61
  206.4 11.7 %cholesky.255 = f32[128,128]{1,0:T(8,128)S(1)} custom-call(f32[128,128]{1,0:T(8,128)S(1)} %convolution_subtract_fusion.5), custom_call_target="Cholesky" | custom-call | tf_op jit(solution)/shard_map/jit(cholesky)/cholesky | solution.py:61
  219.7 9.3 %all-to-all-start.5 = ((f32[12,128,128]{2,1,0:T(8,128)}), f32[12,128,128]{2,1,0:T(8,128)S(1)}, u32[]{:S(2)}, u32[]{:S(2)}) async-start(f32[12,128,128]{2,1,0:T(8,128)} %broadcast_in_dim.11), calls=%async_computation.5 | async-start | bytes 1572864 | tf_op jit(solution)/shard_map/all_to_all | solution.py:11
  234.7 14.0 %while.1 = (s32[]{:T(128)}, f32[512,512]{1,0:T(8,128)}, s32[4,2]{0,1:T(2,128)S(1)}, f32[4,128,128]{2,1,0:T(8,128)}, s32[]{:T(128)}) while((s32[]{:T(128)}, f32[512,512]{1,0:T(8,128)}, s32[4,2]{0,1:T(2,128)S(1)}, f32[4,128,128]{2,1,0:T(8,128)}, s32[]{:T(128)}) %tuple.51), condition=%wide.while_cond, body=%wide.while_body.sunk | while | flops 2 | bytes 132705 | solution.py:63
  235.3 2.9 bitcast_dynamic-update-slice_fusion.2
  238.8 2.9 bitcast_dynamic-update-slice_fusion.2
  242.3 2.9 bitcast_dynamic-update-slice_fusion.2
  245.8 2.8 bitcast_dynamic-update-slice_fusion.2
  248.7 40.1 %custom-call.33 = f32[4,128,128]{1,2,0:T(8,128)S(1)} custom-call(f32[4,128,128]{2,1,0:T(8,128)} %get-tuple-element.14), custom_call_target="InvertDiagBlocksLowerTriangular" | custom-call | tf_op jit(solution)/shard_map/triangular_solve | solution.py:63
  289.9 1.5 fusion.13
  291.4 1.6 convolution_subtract_fusion.1
  293.4 1.9 convolution_subtract_fusion
  295.7 2.4 convolution_subtract_fusion.2
  299.4 6.4 %all-to-all-start.6 = ((f32[64,1,512]{2,1,0:T(1,128)}), f32[64,1,512]{2,1,0:T(1,128)S(1)}, u32[]{:S(2)}, u32[]{:S(2)}) async-start(f32[64,1,512]{2,1,0:T(1,128)} %broadcast_in_dim.12), calls=%async_computation.6 | async-start | bytes 262144 | tf_op jit(solution)/shard_map/all_to_all | solution.py:42
  305.9 1.4 fusion
  307.3 9.7 %all-to-all-done.6 = f32[64,1,512]{2,1,0:T(1,128)S(1)} async-done(((f32[64,1,512]{2,1,0:T(1,128)}), f32[64,1,512]{2,1,0:T(1,128)S(1)}, u32[]{:S(2)}, u32[]{:S(2)}) %all-to-all-start.6) | async-done | bytes 131104 | tf_op jit(solution)/shard_map/all_to_all | solution.py:42
  318.4 1.4 fusion.2
  (113 shorter events, 26.1 us)
Async XLA Ops:
  0.6 1.1 copy-start
  90.7 30.5 %all-to-all-start.3 = ((f32[12,112,128]{2,1,0:T(8,128)}), f32[12,112,128]{2,1,0:T(8,128)S(1)}, u32[]{:S(2)}, u32[]{:S(2)}) async-start(f32[12,112,128]{2,1,0:T(8,128)} %broadcast_in_dim.10), calls=%async_computation.3 | async-start | bytes 1376256 | tf_op jit(solution)/shard_map/all_to_all | solution.py:11
  95.1 1.0 copy-start.2
  95.1 1.1 copy-start.5
  122.8 0.6 copy-start.10
  122.9 0.6 copy-start.12
  123.1 0.9 copy-start.14
  123.1 0.9 copy-start.15
  123.1 0.9 copy-start.16
  123.3 0.9 copy-start.6
  123.3 0.9 copy-start.8
  123.4 0.6 copy-start.17
  126.7 7.0 %copy-start.7 = (f32[128,128]{0,1:T(8,128)S(1)}, f32[128,128]{0,1:T(8,128)}, u32[]{:S(2)}) copy-start(f32[128,128]{0,1:T(8,128)} %get-tuple-element.38) | copy-start | bytes 196612
  126.7 7.0 %copy-start.9 = (f32[128,128]{0,1:T(8,128)S(1)}, f32[128,128]{0,1:T(8,128)}, u32[]{:S(2)}) copy-start(f32[128,128]{0,1:T(8,128)} %get-tuple-element.39) | copy-start | bytes 196612
  126.7 7.0 %copy-start.11 = (f32[128,128]{0,1:T(8,128)S(1)}, f32[128,128]{0,1:T(8,128)}, u32[]{:S(2)}) copy-start(f32[128,128]{0,1:T(8,128)} %copy-done.10) | copy-start | bytes 196612
  126.7 7.0 %copy-start.13 = (f32[128,128]{0,1:T(8,128)S(1)}, f32[128,128]{0,1:T(8,128)}, u32[]{:S(2)}) copy-start(f32[128,128]{0,1:T(8,128)} %copy-done.12) | copy-start | bytes 196612
  126.7 92.0 %all-to-all-start.4 = ((f32[12,128,128]{2,1,0:T(8,128)}), f32[12,128,128]{2,1,0:T(8,128)S(1)}, u32[]{:S(2)}, u32[]{:S(2)}) async-start(f32[12,128,128]{2,1,0:T(8,128)} %reshape_reshape.11), calls=%async_computation.4 | async-start | bytes 1572864 | tf_op jit(solution)/shard_map/all_to_all | solution.py:9
  134.8 1.0 copy-start.1
  219.7 69.1 %all-to-all-start.5 = ((f32[12,128,128]{2,1,0:T(8,128)}), f32[12,128,128]{2,1,0:T(8,128)S(1)}, u32[]{:S(2)}, u32[]{:S(2)}) async-start(f32[12,128,128]{2,1,0:T(8,128)} %broadcast_in_dim.11), calls=%async_computation.5 | async-start | bytes 1572864 | tf_op jit(solution)/shard_map/all_to_all | solution.py:11
  289.9 3.5 %copy-start.4 = (f32[512,512]{1,0:T(8,128)S(1)}, f32[512,512]{1,0:T(8,128)}, u32[]{:S(2)}) copy-start(f32[512,512]{1,0:T(8,128)} %constant_dynamic-update-slice_fusion) | copy-start | bytes 3145732
  298.7 7.2 %copy-start.3 = (f32[128,384]{1,0:T(8,128)S(1)}, f32[128,384]{1,0:T(8,128)}, u32[]{:S(2)}) copy-start(f32[128,384]{1,0:T(8,128)} %param.4) | copy-start | bytes 589828
  299.4 17.5 %all-to-all-start.6 = ((f32[64,1,512]{2,1,0:T(1,128)}), f32[64,1,512]{2,1,0:T(1,128)S(1)}, u32[]{:S(2)}, u32[]{:S(2)}) async-start(f32[64,1,512]{2,1,0:T(1,128)} %broadcast_in_dim.12), calls=%async_computation.6 | async-start | bytes 262144 | tf_op jit(solution)/shard_map/all_to_all | solution.py:42
  317.2 1.2 copy-start.18

commit v5 on v4

--- a/solution.py
+++ b/solution.py
@@ -37,6 +37,27 @@
     return jnp.concatenate(rows, axis=0)
 
 
+def lower_inverse(factor):
+    size = factor.shape[0]
+    levels = [factor[None]]
+    while levels[-1].shape[-1] > 1:
+        blocks = levels[-1]
+        half = blocks.shape[-1] // 2
+        pair = jnp.stack([blocks[:, :half, :half], blocks[:, half:, half:]], axis=1)
+        levels.append(pair.reshape(-1, half, half))
+    inverse = 1.0 / levels[-1]
+    for blocks in reversed(levels[:-1]):
+        width = blocks.shape[-1] // 2
+        upper = inverse[0::2]
+        lower = inverse[1::2]
+        corner = blocks[:, width:, :width]
+        off = -jnp.matmul(jnp.matmul(lower, corner, precision=lax.Precision.HIGHEST), upper, precision=lax.Precision.HIGHEST)
+        top = jnp.concatenate([upper, jnp.zeros_like(upper)], axis=2)
+        bottom = jnp.concatenate([off, lower], axis=2)
+        inverse = jnp.concatenate([top, bottom], axis=1)
+    return inverse[0]
+
+
 def gather_psum(x, axis, size):
     copies = jnp.broadcast_to(x[None], (size,) + x.shape)
     return jnp.sum(lax.all_to_all(copies, axis, 0, 0, tiled=False), axis=0)
@@ -60,9 +81,8 @@
     gram_matrix = symmetric_from_lower_blocks(gram_blocks, rank // block)
     factor = jnp.linalg.cholesky(gram_matrix)
     rows = panel_full.shape[0]
-    solved = lax.linalg.triangular_solve(
-        factor, jnp.concatenate([panel_full, cross], axis=0), left_side=False, lower=True, transpose_a=True
-    )
+    inverse = lower_inverse(factor)
+    solved = jnp.dot(jnp.concatenate([panel_full, cross], axis=0), inverse.T, precision=highest)
     orthonormal = solved[:rows]
     right_factor = solved[rows:]
     col_sumsq = gather_psum(jnp.sum(right_factor * right_factor, axis=0), "tensor", tensor_size)

time: 326 us -> 330 us (1.012)
  waiting for transfers between devices: 33 us -> 81.3 us
  other arithmetic: 122 us -> 84.4 us
  local copies, waits for them, and re-layouts: 27.7 us -> 22.8 us
    another operation x3 -> x7, other arithmetic: 41.3 us -> 0.31 us  [lower_inverse(): pair = jnp.stack([blocks[:, :half, :half], blocks[:, half:, half:]], axis=1)]
    all_to_all x2, waiting for transfers between devices: 23.3 us -> 48.8 us  [scatter_gather_psum(): return lax.all_to_all(spread, axis, 0, 0, tiled=False).reshape(x.shape)]
    all_to_all x1, waiting for transfers between devices: 0.01 us -> 23 us  [scatter_gather_psum(): mine = jnp.sum(lax.all_to_all(chunks, axis, 0, 0, tiled=False), axis=0)]
    another operation x13 -> x16, local copies, waits for them, and re-layouts: 14 us -> 2.63 us  [lower_inverse(): pair = jnp.stack([blocks[:, :half, :half], blocks[:, half:, half:]], axis=1)]
    dot_general x0 -> x17, matrix products: none -> 10.5 us  [the longest x8 4.23 us: lower_inverse(): jnp.matmul(lower, corner, precision=lax.Precision.HIGHEST)]
    another operation x7 -> x0, matrix products: 8.56 us -> none  [local(): lax.linalg.triangular_solve(factor, jnp.concatenate([panel_full, cross],...]
    unnamed x49 -> x65, local copies, waits for them, and re-layouts: 5.3 us -> 9.98 us
    another operation x6, matrix products: 5.47 us -> 1.87 us  [local(): factor = jnp.linalg.cholesky(gram_matrix)]
  transfers between devices with their start and end apart: 4 -> 4, of which waited for: 2 -> 4; matrix products, arithmetic and copies ran while one was open for 45% -> 3% of each run, Pallas kernels for 0% -> 0%
where the time goes in v5:
time: 330 us; the launch traced here: 326 us
  blocking collectives  84.9 us (26%)
  other arithmetic  84.4 us (26%)
  waiting for transfers between devices  81.3 us (25%)
  starting transfers between devices  28 us (8%)
  local copies, waits for them, and re-layouts  22.8 us (7%)
  matrix products  19.8 us (6%)
  between operations  4.32 us (1%)
    another operation x15, other arithmetic, local(): factor = jnp.linalg.cholesky(gram_matrix)  79.3 us
    all_to_all x2, blocking collectives, scatter_gather_psum(): mine = jnp.sum(lax.all_to_all(chunks, axis, 0, 0, tiled=False), axis=0)  67.2 us
    all_to_all x2, waiting for transfers between devices, scatter_gather_psum(): return lax.all_to_all(spread, axis, 0, 0, tiled=False).reshape(x.shape)  48.8 us
    all_to_all x1, waiting for transfers between devices, scatter_gather_psum(): mine = jnp.sum(lax.all_to_all(chunks, axis, 0, 0, tiled=False), axis=0)  23 us
    all_to_all x1, blocking collectives, scatter_gather_psum(): return lax.all_to_all(spread, axis, 0, 0, tiled=False).reshape(x.shape)  17.7 us
    all_to_all x2, starting transfers between devices, scatter_gather_psum(): return lax.all_to_all(spread, axis, 0, 0, tiled=False).reshape(x.shape)  12.1 us
    unnamed x65, local copies, waits for them, and re-layouts  9.98 us
    all_to_all x1, waiting for transfers between devices, gather_psum(): return jnp.sum(lax.all_to_all(copies, axis, 0, 0, tiled=False), axis=0)  9.58 us
  transfers between devices with their start and end apart: 4, of which 4 were waited for; matrix products, arithmetic and copies ran while one was open for 3% of the time, Pallas kernels for 0%

profile of v5, /device:TPU:1, one launch (start us, length us, event | category | flops | bytes accessed | tf_op | source)
XLA Modules:
  0.0 325.6 jit_solution(9215448760010575898)
XLA Ops:
  0.6 1.1 copy-done
  1.8 1.6 fusion.44
  3.4 27.0 %all_to_all.36 = f32[64,8,128]{2,1,0:T(8,128)S(1)} all-to-all(f32[64,8,128]{2,1,0:T(8,128)S(1)} %reshape.112), channel_id=1, replica_groups=mesh['fsdp'=12,'tensor'=64] {'tensor'}, dimensions={0} | all-to-all | bytes 524288 | tf_op jit(solution)/shard_map/all_to_all | solution.py:9
  30.5 17.7 %all_to_all.37 = f32[64,8,128]{2,1,0:T(8,128)S(1)} all-to-all(f32[64,8,128]{2,1,0:T(8,128)S(1)} %broadcast_in_dim.11), channel_id=1, replica_groups=mesh['fsdp'=12,'tensor'=64] {'tensor'}, dimensions={0} | all-to-all | bytes 524288 | tf_op jit(solution)/shard_map/all_to_all | solution.py:11
  48.3 1.0 fusion.87
  49.6 40.2 %all_to_all.38 = f32[12,112,128]{2,1,0:T(8,128)S(1)} all-to-all(f32[12,112,128]{2,1,0:T(8,128)S(1)} %bitcast.193), channel_id=1, replica_groups=mesh['fsdp'=12,'tensor'=64] {'fsdp'}, dimensions={0} | all-to-all | bytes 1376256 | tf_op jit(solution)/shard_map/all_to_all | solution.py:9
  90.7 5.0 %all-to-all-start.3 = ((f32[12,112,128]{2,1,0:T(8,128)}), f32[12,112,128]{2,1,0:T(8,128)S(1)}, u32[]{:S(2)}, u32[]{:S(2)}) async-start(f32[12,112,128]{2,1,0:T(8,128)} %broadcast_in_dim.12), calls=%async_computation.3 | async-start | bytes 1376256 | tf_op jit(solution)/shard_map/all_to_all | solution.py:11
  95.8 1.7 fusion.43
  97.5 23.9 %all-to-all-done.3 = f32[12,112,128]{2,1,0:T(8,128)S(1)} async-done(((f32[12,112,128]{2,1,0:T(8,128)}), f32[12,112,128]{2,1,0:T(8,128)S(1)}, u32[]{:S(2)}, u32[]{:S(2)}) %all-to-all-start.3) | async-done | bytes 688160 | tf_op jit(solution)/shard_map/all_to_all | solution.py:11
  123.7 1.0 maximum_maximum_fusion
  125.0 1.2 fusion.14
  127.3 11.7 %cholesky.104 = f32[128,128]{1,0:T(8,128)S(1)} custom-call(f32[128,128]{1,0:T(8,128)S(1)} %cholesky.266), custom_call_target="Cholesky" | custom-call | tf_op jit(solution)/shard_map/jit(cholesky)/cholesky | solution.py:82
  139.8 9.8 %custom-call.27 = f32[1,128,128]{1,2,0:T(8,128)S(1)} custom-call(f32[1,128,128]{2,1,0:T(8,128)S(1)} %get-tuple-element.62), custom_call_target="InvertDiagBlocksLowerTriangular" | custom-call | tf_op jit(solution)/shard_map/jit(cholesky)/cholesky | solution.py:82
  150.3 11.9 %cholesky.217 = f32[128,128]{1,0:T(8,128)S(1)} custom-call(f32[128,128]{1,0:T(8,128)S(1)} %cholesky.270), custom_call_target="Cholesky" | custom-call | tf_op jit(solution)/shard_map/jit(cholesky)/cholesky | solution.py:82
  162.8 9.8 %custom-call.28 = f32[1,128,128]{1,2,0:T(8,128)S(1)} custom-call(f32[1,128,128]{2,1,0:T(8,128)S(1)} %get-tuple-element.59), custom_call_target="InvertDiagBlocksLowerTriangular" | custom-call | tf_op jit(solution)/shard_map/jit(cholesky)/cholesky | solution.py:82
  173.3 11.7 %cholesky.238 = f32[128,128]{1,0:T(8,128)S(1)} custom-call(f32[128,128]{1,0:T(8,128)S(1)} %cholesky.275), custom_call_target="Cholesky" | custom-call | tf_op jit(solution)/shard_map/jit(cholesky)/cholesky | solution.py:82
  185.7 9.8 %custom-call.29 = f32[1,128,128]{1,2,0:T(8,128)S(1)} custom-call(f32[1,128,128]{2,1,0:T(8,128)S(1)} %get-tuple-element.56), custom_call_target="InvertDiagBlocksLowerTriangular" | custom-call | tf_op jit(solution)/shard_map/jit(cholesky)/cholesky | solution.py:82
  196.1 11.9 %cholesky.255 = f32[128,128]{1,0:T(8,128)S(1)} custom-call(f32[128,128]{1,0:T(8,128)S(1)} %convolution_subtract_fusion.2), custom_call_target="Cholesky" | custom-call | tf_op jit(solution)/shard_map/jit(cholesky)/cholesky | solution.py:82
  215.9 1.7 copy.293
  219.2 1.0 fusion.41
  222.0 1.2 select_maximum_fusion.7
  225.5 6.3 %all-to-all-start.4 = ((f32[12,128,128]{2,1,0:T(8,128)}), f32[12,128,128]{2,1,0:T(8,128)S(1)}, u32[]{:S(2)}, u32[]{:S(2)}) async-start(f32[12,128,128]{2,1,0:T(8,128)} %reshape_reshape.11), calls=%async_computation.4 | async-start | bytes 1572864 | tf_op jit(solution)/shard_map/all_to_all | solution.py:9
  237.5 23.0 %all-to-all-done.4 = f32[12,128,128]{2,1,0:T(8,128)S(1)} async-done(((f32[12,128,128]{2,1,0:T(8,128)}), f32[12,128,128]{2,1,0:T(8,128)S(1)}, u32[]{:S(2)}, u32[]{:S(2)}) %all-to-all-start.4) | async-done | bytes 786464 | tf_op jit(solution)/shard_map/all_to_all | solution.py:9
  261.5 7.1 %all-to-all-start.5 = ((f32[12,128,128]{2,1,0:T(8,128)}), f32[12,128,128]{2,1,0:T(8,128)S(1)}, u32[]{:S(2)}, u32[]{:S(2)}) async-start(f32[12,128,128]{2,1,0:T(8,128)} %broadcast_in_dim.13), calls=%async_computation.5 | async-start | bytes 1572864 | tf_op jit(solution)/shard_map/all_to_all | solution.py:11
  269.3 1.2 fusion.27
  272.3 24.9 %all-to-all-done.5 = f32[12,128,128]{2,1,0:T(8,128)S(1)} async-done(((f32[12,128,128]{2,1,0:T(8,128)}), f32[12,128,128]{2,1,0:T(8,128)S(1)}, u32[]{:S(2)}, u32[]{:S(2)}) %all-to-all-start.5) | async-done | bytes 786464 | tf_op jit(solution)/shard_map/all_to_all | solution.py:11
  297.2 1.0 reshape_reshape_reshape.3
  298.2 3.0 fusion.5
  302.1 9.5 %all-to-all-start.6 = ((f32[64,1,512]{2,1,0:T(1,128)}), f32[64,1,512]{2,1,0:T(1,128)S(1)}, u32[]{:S(2)}, u32[]{:S(2)}) async-start(f32[64,1,512]{2,1,0:T(1,128)} %broadcast_in_dim.15), calls=%async_computation.6 | async-start | bytes 262144 | tf_op jit(solution)/shard_map/all_to_all | solution.py:63
  311.7 1.5 fusion.1
  313.2 9.6 %all-to-all-done.6 = f32[64,1,512]{2,1,0:T(1,128)S(1)} async-done(((f32[64,1,512]{2,1,0:T(1,128)}), f32[64,1,512]{2,1,0:T(1,128)S(1)}, u32[]{:S(2)}, u32[]{:S(2)}) %all-to-all-start.6) | async-done | bytes 131104 | tf_op jit(solution)/shard_map/all_to_all | solution.py:63
  323.8 1.5 fusion.3
  (169 shorter events, 30.5 us)
Async XLA Ops:
  0.6 1.1 copy-start
  90.7 5.0 %copy-start.5 = (f32[128,384]{1,0:T(8,128)S(1)}, f32[128,384]{1,0:T(8,128)}, u32[]{:S(2)}) copy-start(f32[128,384]{1,0:T(8,128)} %param.4) | copy-start | bytes 589828
  90.7 5.0 %copy-start.16 = (bf16[128,384]{1,0:T(8,128)(2,1)S(1)}, bf16[128,384]{1,0:T(8,128)(2,1)}, u32[]{:S(2)}) copy-start(bf16[128,384]{1,0:T(8,128)(2,1)} %param.5) | copy-start | bytes 294916
  90.7 30.6 %all-to-all-start.3 = ((f32[12,112,128]{2,1,0:T(8,128)}), f32[12,112,128]{2,1,0:T(8,128)S(1)}, u32[]{:S(2)}, u32[]{:S(2)}) async-start(f32[12,112,128]{2,1,0:T(8,128)} %broadcast_in_dim.12), calls=%async_computation.3 | async-start | bytes 1376256 | tf_op jit(solution)/shard_map/all_to_all | solution.py:11
  122.4 1.3 copy-start.18
  122.4 1.3 copy-start.19
  122.5 1.2 copy-start.23
  122.7 0.9 copy-start.20
  122.8 0.9 copy-start.21
  122.8 0.9 copy-start.22
  126.3 1.0 copy-start.3
  127.3 22.3 %copy-start.4 = (f32[512,512]{1,0:T(8,128)S(1)}, f32[512,512]{1,0:T(8,128)}, u32[]{:S(2)}) copy-start(f32[512,512]{1,0:T(8,128)} %copy-done.3) | copy-start | bytes 3145732
  211.4 0.8 copy-start.15
  212.2 0.7 copy-start.7
  213.0 0.7 copy-start.9
  213.8 0.7 copy-start.11
  214.5 0.7 copy-start.13
  220.4 0.7 copy-start.24
  222.0 2.5 copy-start.2
  225.5 35.0 %all-to-all-start.4 = ((f32[12,128,128]{2,1,0:T(8,128)}), f32[12,128,128]{2,1,0:T(8,128)S(1)}, u32[]{:S(2)}, u32[]{:S(2)}) async-start(f32[12,128,128]{2,1,0:T(8,128)} %reshape_reshape.11), calls=%async_computation.4 | async-start | bytes 1572864 | tf_op jit(solution)/shard_map/all_to_all | solution.py:9
  231.8 0.9 copy-start.25
  232.7 0.9 copy-start.14
  234.4 1.0 copy-start.12
  235.9 1.0 copy-start.10
  261.5 7.1 %copy-start.8 = (f32[2,2,128,128]{3,2,1,0:T(8,128)S(1)}, f32[2,2,128,128]{3,2,1,0:T(8,128)}, u32[]{:S(2)}) copy-start(f32[2,2,128,128]{3,2,1,0:T(8,128)} %copy-done.7) | copy-start | bytes 786436
  261.5 35.8 %all-to-all-start.5 = ((f32[12,128,128]{2,1,0:T(8,128)}), f32[12,128,128]{2,1,0:T(8,128)S(1)}, u32[]{:S(2)}, u32[]{:S(2)}) async-start(f32[12,128,128]{2,1,0:T(8,128)} %broadcast_in_dim.13), calls=%async_computation.5 | async-start | bytes 1572864 | tf_op jit(solution)/shard_map/all_to_all | solution.py:11
  301.4 10.3 %copy-start.6 = (f32[128,384]{1,0:T(8,128)S(1)}, f32[128,384]{1,0:T(8,128)}, u32[]{:S(2)}) copy-start(f32[128,384]{1,0:T(8,128)} %param.4) | copy-start | bytes 589828
  302.1 9.6 %copy-start.17 = (bf16[128,384]{1,0:T(8,128)(2,1)S(1)}, bf16[128,384]{1,0:T(8,128)(2,1)}, u32[]{:S(2)}) copy-start(bf16[128,384]{1,0:T(8,128)(2,1)} %param.5) | copy-start | bytes 294916
  302.1 20.7 %all-to-all-start.6 = ((f32[64,1,512]{2,1,0:T(1,128)}), f32[64,1,512]{2,1,0:T(1,128)S(1)}, u32[]{:S(2)}, u32[]{:S(2)}) async-start(f32[64,1,512]{2,1,0:T(1,128)} %broadcast_in_dim.15), calls=%async_computation.6 | async-start | bytes 262144 | tf_op jit(solution)/shard_map/all_to_all | solution.py:63
  322.9 0.9 copy-start.26
  323.8 1.5 copy-start.1
